TPU v7x, 128 devices: a whole 4x4x4 slice. The times are simulated.
128 devices in a mesh: section: 16 (over y, z_lo, core), sp: 8 (over z_hi, x).
Axes of the slice: x: 4, y: 4, z: 4 (z_hi: 2, z_lo: 2; z = z_hi * 2 + z_lo), core: 2. Of those that a mesh axis runs over, the one named last changes fastest.
Arguments:
- resid: float32 [16, 896, 6144], P('section', 'sp'), may hold values from -1.8 to 1.8
- qkv: bfloat16 [16, 896, 3, 6144], P('section', 'sp'), may hold values from -48 to 48
- cache_kv: bfloat16 [16, 2, 2, 1344, 6144], P('section', None, None, None, 'sp'), may hold values from -6 to 6
- out_proj: bfloat16 [16, 6144, 6144], P('section', 'sp'), may hold values from -0.078125 to 0.078125
- gate: float32 [16, 2, 6144], P('section'), may hold values from 0.5 to 2
- span_ids: int32 [16], P('section'), may hold values from 3 to 39
- cache_counts: int32 [16], P('section'), may hold values from 0 to 3, as said below
- span_mask: int32 [40, 40], replicated, may hold values from 0 to 1, as said below
Outputs:
- carried: float32 [16, 896, 6144], P('section', 'sp')
Inputs may be any that keep to these rules, and one draw needn't show every extreme that they name: `cache_counts`: some section has all 3 slots filled. span_mask[i][j] is 0 for j > i and 1 for j = i.
All inputs are finite; a program needn't handle non-finite values.
Results may differ from a plain program's by a relative error of at most 0.006.
Values may be sent and summed in bfloat16 or wider, within the bound.
No kernel may reach another device: no remote copies, remote signals or barrier semaphores. Data moves between devices by JAX's collectives and lax.ppermute only.
A program may use at most 384 MiB of HBM per device.

v0:
```python
import jax
import jax.numpy as jnp
from jax import lax
from jax.sharding import PartitionSpec as P

HDIM = 128
SPAN = 448
NCHUNK = 40
SLOTS = 3
VIDS = 2
TOKS = 896
KEYS = 1344


def passed_along(shard, axis, by):
    devices = lax.axis_size(axis)
    return lax.ppermute(shard, axis, [(i, (i + by) % devices) for i in range(devices)])


def visible_slots(span_id, filled, span_mask):
    row_mask = lax.dynamic_index_in_dim(span_mask, span_id, 0, keepdims=False)
    slot_ids = jnp.arange(SLOTS, dtype=jnp.int32)
    wanted = span_id - 1 - slot_ids
    columns = jnp.arange(NCHUNK, dtype=jnp.int32)
    looked = jnp.sum(jnp.where(columns[None, :] == wanted[:, None], row_mask[None, :], 0), axis=1)
    return (slot_ids < filled) & (looked == 1)


def far_scores(queries, cache_keys, live_slots):
    score_scale = HDIM ** (-0.5)
    scores = (
        jnp.einsum("qhe,khe->hqk", queries, cache_keys, preferred_element_type=jnp.float32)
        * score_scale
    )
    key_live = jnp.repeat(live_slots, SPAN)
    result = jnp.where(key_live[None, None, :], scores, -jnp.inf)
    return result


def mix_video(far_part, queries, own_keys, own_values, cache_values):
    score_scale = HDIM ** (-0.5)
    near_part = (
        jnp.einsum("qhe,khe->hqk", queries, own_keys, preferred_element_type=jnp.float32)
        * score_scale
    )
    scores = jnp.concatenate([far_part, near_part], axis=2)
    highest = jnp.max(scores, axis=2, keepdims=True)
    raised = jnp.exp(scores - highest)
    weights = (raised / jnp.sum(raised, axis=2, keepdims=True)).astype(jnp.bfloat16)
    values_all = jnp.concatenate([cache_values, own_values], axis=0)
    mixed = jnp.einsum("hqk,khe->qhe", weights, values_all, preferred_element_type=jnp.float32)
    return mixed.astype(jnp.bfloat16).reshape(SPAN, queries.shape[1] * HDIM)


def per_device(resid, qkv, cache_kv, out_proj, gate, span_ids, cache_counts, span_mask):
    own_rows = resid.shape[1]
    local_width = cache_kv.shape[4]
    local_heads = local_width // HDIM
    filled = cache_counts[0]
    live_slots = visible_slots(span_ids[0], filled, span_mask)
    cache_keys = cache_kv[0, 0].reshape(VIDS, KEYS, local_heads, HDIM)
    cache_values = cache_kv[0, 1].reshape(VIDS, KEYS, local_heads, HDIM)

    def score_video(inputs_one):
        return far_scores(inputs_one[0], inputs_one[1], live_slots)

    spread = lax.all_to_all(qkv[0], "sp", split_axis=2, concat_axis=0, tiled=True)
    queries = spread[:, 0].reshape(VIDS, SPAN, local_heads, HDIM)
    far_all = lax.map(score_video, (queries, cache_keys))
    own_keys = spread[:, 1].reshape(VIDS, SPAN, local_heads, HDIM)
    own_values = spread[:, 2].reshape(VIDS, SPAN, local_heads, HDIM)

    def mix_one(inputs_one):
        return mix_video(inputs_one[0], inputs_one[1], inputs_one[2], inputs_one[3], inputs_one[4])

    heads_all = lax.map(mix_one, (far_all, queries, own_keys, own_values, cache_values)).reshape(
        TOKS, local_width
    )
    projected = lax.psum_scatter(
        jnp.dot(heads_all, out_proj[0], preferred_element_type=jnp.float32),
        "sp",
        scatter_dimension=0,
        tiled=True,
    )
    device_place = lax.axis_index("sp")
    video_of = (device_place * own_rows + jnp.arange(own_rows, dtype=jnp.int32)) // SPAN
    picker = (video_of[:, None] == jnp.arange(VIDS, dtype=jnp.int32)[None, :]).astype(jnp.float32)
    gains = jnp.dot(picker, gate[0], precision=lax.Precision.HIGHEST)
    layer_out = resid[0] + gains * projected
    return passed_along(layer_out[None], "section", 1)


def solution(mesh):
    in_specs = (
        P("section", "sp", None),
        P("section", "sp", None, None),
        P("section", None, None, None, "sp"),
        P("section", "sp", None),
        P("section", None, None),
        P("section"),
        P("section"),
        P(),
    )
    out_specs = P("section", "sp", None)
    return jax.shard_map(
        per_device, mesh=mesh, in_specs=in_specs, out_specs=out_specs, check_vma=False
    )
```

profile of v0, /device:TPU:6, one launch (start us, length us, event | category | flops | bytes accessed | tf_op | source)
XLA Modules:
  0.0 541.8 jit_solution(14017527695531019002)
XLA Ops:
  6.5 10.0 %copy.53 = bf16[1,112,3,6144]{1,2,3,0:T(4,128)(2,1)} copy(bf16[1,112,3,6144]{3,1,2,0:T(8,128)(2,1)} %param.13) | data formatting | bytes 8257536 | tf_op args[1]
  16.5 8.1 %all-to-all-start = ((bf16[112,3,6144]{0,1,2:T(4,128)(2,1)}), bf16[112,3,6144]{0,1,2:T(4,128)(2,1)}, u32[]{:S(2)}, u32[]{:S(2)}) async-start(bf16[112,3,6144]{0,1,2:T(4,128)(2,1)} %bitcast.81), calls=%async_computation | async-start | bytes 12582912 | tf_op jit(solution)/shard_map/all_to_all | solution.py:67
  25.9 5.7 %fusion.31 = (bf16[1,1,2,1344,768]{4,3,2,1,0:T(8,128)(2,1)}, bf16[1,1,2,1344,768]{4,3,2,1,0:T(8,128)(2,1)}) fusion(bf16[1,2,2,1344,768]{4,3,2,1,0:T(8,128)(2,1)} %param.14), kind=kLoop, calls=%fused_computation.44 | loop fusion | bytes 16515072 | tf_op jit(solution)/shard_map/slice | solution.py:61
  31.6 6.4 %copy.58 = bf16[1,1,2,1344,768]{3,4,2,1,0:T(8,128)(2,1)} copy(bf16[1,1,2,1344,768]{4,3,2,1,0:T(8,128)(2,1)} %get-tuple-element.147) | data formatting | bytes 8257536 | tf_op jit(solution)/shard_map/slice | solution.py:61
  38.1 6.4 %copy.60 = bf16[2,1344,6,128]{3,1,2,0:T(8,128)(2,1)} copy(bf16[2,1344,6,128]{1,3,2,0:T(8,128)(2,1)} %bitcast.82) | data formatting | bytes 8257536 | tf_op jit(solution)/shard_map/while | solution.py:69
  44.5 6.4 %copy.52 = bf16[1,1,2,1344,768]{3,4,2,1,0:T(8,128)(2,1)} copy(bf16[1,1,2,1344,768]{4,3,2,1,0:T(8,128)(2,1)} %get-tuple-element.148) | data formatting | bytes 8257536 | tf_op jit(solution)/shard_map/slice | solution.py:62
  50.9 6.4 %copy.62 = bf16[2,1344,6,128]{3,1,2,0:T(8,128)(2,1)} copy(bf16[2,1344,6,128]{1,3,2,0:T(8,128)(2,1)} %bitcast.83) | data formatting | bytes 8257536 | tf_op jit(solution)/shard_map/while | solution.py:76
  57.4 0.7 dynamic-slice_bitcast_fusion.3
  58.1 0.2 select_reduce_fusion
  58.3 59.0 %all-to-all-done = bf16[112,3,6144]{0,1,2:T(4,128)(2,1)} async-done(((bf16[112,3,6144]{0,1,2:T(4,128)(2,1)}), bf16[112,3,6144]{0,1,2:T(4,128)(2,1)}, u32[]{:S(2)}, u32[]{:S(2)}) %all-to-all-start) | async-done | bytes 4128800 | tf_op jit(solution)/shard_map/all_to_all | solution.py:67
  117.3 10.0 %copy.68 = bf16[112,3,8,768]{3,0,2,1:T(8,128)(2,1)} copy(bf16[112,3,8,768]{0,1,3,2:T(4,128)(2,1)} %bitcast.14) | data formatting | bytes 8257536 | tf_op jit(solution)/shard_map/all_to_all | solution.py:67
  127.3 3.5 fusion.32
  130.8 2.5 reshape.32
  133.3 1.7 copy.59
  135.0 18.4 %while.20 = (s32[]{:T(128)}, f32[2,6,448,1344]{3,2,1,0:T(8,128)}, pred[3]{0:T(512)(128)(4,1)S(1)}, bf16[2,448,6,128]{3,1,2,0:T(8,128)(2,1)S(1)}, bf16[2,1344,6,128]{3,1,2,0:T(8,128)(2,1)}, /*index=5*/s32[]{:T(128)}) while((s32[]{:T(128)}, f32[2,6,448,1344]{3,2,1,0:T(8,128)}, pred[3]{0:T(512)(128)(4,1)S(1)}, ...), condition=%wide.region_2.3_spmd, body=%wide.region_1.2_spmd.sunk | while | flops 932069376 | bytes 17899016 | solution.py:69
  135.1 0.1 broadcast_in_dim.72
  135.2 9.0 %bitcast_dynamic-update-slice_fusion.2 = f32[2,6,448,1344]{3,2,1,0:T(8,128)} fusion(f32[2,6,448,1344]{3,2,1,0:T(8,128)} %get-tuple-element.241, s32[]{:T(128)} %get-tuple-element.240, pred[1344]{0:T(1024)(128)(4,1)S(1)} %broadcast_in_dim.72, bf16[2,1344,6,128]{3,1,2,0:T(8,128)(2,1)} %get-tuple-element.250, ...), kind=kOutput, calls=%fused_computation.clone.1 | convolution fusion | flops 932069376 | bytes 17894912 | tf_op jit(solution)/shard_map/while/body/eval_jaxpr/qhe,khe->hqk/dot_general | solution.py:32
  144.3 9.0 %bitcast_dynamic-update-slice_fusion.2 = f32[2,6,448,1344]{3,2,1,0:T(8,128)} fusion(f32[2,6,448,1344]{3,2,1,0:T(8,128)} %get-tuple-element.241, s32[]{:T(128)} %get-tuple-element.240, pred[1344]{0:T(1024)(128)(4,1)S(1)} %broadcast_in_dim.72, bf16[2,1344,6,128]{3,1,2,0:T(8,128)(2,1)} %get-tuple-element.250, ...), kind=kOutput, calls=%fused_computation.clone.1 | convolution fusion | flops 932069376 | bytes 17894912 | tf_op jit(solution)/shard_map/while/body/eval_jaxpr/qhe,khe->hqk/dot_general | solution.py:32
  153.4 4.1 reshape.30
  157.5 2.8 copy.63
  160.3 2.5 reshape.31
  162.8 2.8 copy.65
  165.6 81.0 %while.21 = (s32[]{:T(128)}, bf16[2,448,768]{2,1,0:T(8,128)(2,1)}, bf16[2,1344,6,128]{3,1,2,0:T(8,128)(2,1)}, bf16[2,448,6,128]{3,1,2,0:T(8,128)(2,1)}, f32[2,6,...) while((s32[]{:T(128)}, bf16[2,448,768]{2,1,0:T(8,128)(2,1)}, ...), condition=%wide.region_7.8_spmd, body=%wide.region_3.7_spmd.sunk | while | flops 1586989824 | bytes 108822680 | solution.py:76
  165.6 4.4 fusion.43
  169.9 11.6 %dynamic-slice_reduce_fusion.2 = (f32[6,448]{1,0:T(8,128)S(1)}, f32[6,448,1344]{2,1,0:T(8,128)}) fusion(f32[2,6,448,1344]{3,2,1,0:T(8,128)} %get-tuple-element.272, s32[]{:T(128)} %get-tuple-element.260), kind=kLoop, calls=%fused_computation.9.clone.1 | loop fusion | flops 3609984 | bytes 28912132 | tf_op jit(solution)/shard_map/while/body/eval_jaxpr/reduce_max | solution.py:47
  181.6 10.8 %fusion.44 = f32[6,448]{1,0:T(8,128)S(1)} fusion(f32[6,448,448]{2,1,0:T(8,128)} %get-tuple-element.230, f32[6,448,1344]{2,1,0:T(8,128)} %get-tuple-element.231, f32[6,448]{1,0:T(8,128)S(1)} %reduce_max.27), kind=kLoop, calls=%fused_computation.11.clone.1 | loop fusion | flops 14448000 | bytes 19289088 | tf_op jit(solution)/shard_map/while/body/eval_jaxpr/reduce_sum | solution.py:49
  192.4 0.1 dynamic-slice_bitcast_fusion.7
  192.5 1.2 copy-done.2
  193.7 0.9 dynamic-slice_bitcast_fusion.6
  194.6 10.0 %fusion.45 = bf16[448,6,128]{2,0,1:T(8,128)(2,1)S(1)} fusion(bf16[448,6,128]{2,0,1:T(8,128)(2,1)} %dynamic-slice_bitcast_fusion.6, bf16[1344,6,128]{2,0,1:T(8,128)(2,1)S(1)} %dynamic-slice_bitcast_fusion.7, f32[6,448,448]{2,1,0:T(8,128)} %get-tuple-element.230, f32[6,448,1344]{2,1,0:T(8,128)} %get-tuple-element.231, f32[6,448]{1,0:T(8,128)S(1)} %fusion.44, ...), kind=kOutput, calls=%fused_computation.19.clone.1 | convolution fusion | flops 1258242048 | bytes 22729728 | tf_op jit(solution)/shard_map/while/body/eval_jaxpr/hqk,khe->qhe/dot_general | solution.py:51
  204.6 0.3 copy.79
  204.9 0.3 copy.80
  205.2 0.9 constant_dynamic-update-slice_fusion.2
  206.1 4.4 fusion.43
  210.5 11.6 %dynamic-slice_reduce_fusion.2 = (f32[6,448]{1,0:T(8,128)S(1)}, f32[6,448,1344]{2,1,0:T(8,128)}) fusion(f32[2,6,448,1344]{3,2,1,0:T(8,128)} %get-tuple-element.272, s32[]{:T(128)} %get-tuple-element.260), kind=kLoop, calls=%fused_computation.9.clone.1 | loop fusion | flops 3609984 | bytes 28912132 | tf_op jit(solution)/shard_map/while/body/eval_jaxpr/reduce_max | solution.py:47
  222.1 10.8 %fusion.44 = f32[6,448]{1,0:T(8,128)S(1)} fusion(f32[6,448,448]{2,1,0:T(8,128)} %get-tuple-element.230, f32[6,448,1344]{2,1,0:T(8,128)} %get-tuple-element.231, f32[6,448]{1,0:T(8,128)S(1)} %reduce_max.27), kind=kLoop, calls=%fused_computation.11.clone.1 | loop fusion | flops 14448000 | bytes 19289088 | tf_op jit(solution)/shard_map/while/body/eval_jaxpr/reduce_sum | solution.py:49
  232.9 0.1 dynamic-slice_bitcast_fusion.7
  233.1 1.2 copy-done.2
  234.2 0.9 dynamic-slice_bitcast_fusion.6
  235.1 10.0 %fusion.45 = bf16[448,6,128]{2,0,1:T(8,128)(2,1)S(1)} fusion(bf16[448,6,128]{2,0,1:T(8,128)(2,1)} %dynamic-slice_bitcast_fusion.6, bf16[1344,6,128]{2,0,1:T(8,128)(2,1)S(1)} %dynamic-slice_bitcast_fusion.7, f32[6,448,448]{2,1,0:T(8,128)} %get-tuple-element.230, f32[6,448,1344]{2,1,0:T(8,128)} %get-tuple-element.231, f32[6,448]{1,0:T(8,128)S(1)} %fusion.44, ...), kind=kOutput, calls=%fused_computation.19.clone.1 | convolution fusion | flops 1258242048 | bytes 22729728 | tf_op jit(solution)/shard_map/while/body/eval_jaxpr/hqk,khe->qhe/dot_general | solution.py:51
  245.2 0.3 copy.79
  245.5 0.3 copy.80
  245.7 0.9 constant_dynamic-update-slice_fusion.2
  246.6 16.9 %fusion.24 = f32[896,6144]{1,0:T(8,128)} fusion(bf16[896,768]{1,0:T(8,128)(2,1)} %bitcast.85, bf16[1,768,6144]{2,1,0:T(8,128)(2,1)} %param.15), kind=kOutput, calls=%fused_computation.29 | convolution fusion | flops 8455716864 | bytes 32833536 | tf_op jit(solution)/shard_map/dot_general | solution.py:80
  263.6 231.9 %reduce-scatter.2.cloned.1.call-done = f32[112,6144]{1,0:T(8,128)} async-done(((f32[896,6144]{1,0:T(8,128)}), f32[112,6144]{1,0:T(8,128)}) %reduce-scatter.2.cloned.1.call-update) | async-done | bytes 2752528 | tf_op jit(solution)/shard_map/reduce_scatter | solution.py:79
  495.5 3.3 fusion.27
  498.9 34.6 %collective-permute-done = f32[1,112,6144]{2,1,0:T(8,128)S(1)} collective-permute-done((f32[1,112,6144]{2,1,0:T(8,128)S(1)}, f32[1,112,6144]{2,1,0:T(8,128)S(1)}, u32[]{:S(2)}, u32[]{:S(2)}) %collective-permute-start) | collective-permute-done | bytes 2752544 | tf_op jit(solution)/shard_map/ppermute | solution.py:17
  533.4 1.5 copy.100
  (23 shorter events, 0.4 us)
Async XLA Ops:
  6.5 488.9 %copy-start = (f32[1,2,6144]{2,1,0:T(2,128)S(1)}, f32[1,2,6144]{2,1,0:T(2,128)}, u32[]{:S(2)}) copy-start(f32[1,2,6144]{2,1,0:T(2,128)} %param.16) | copy-start | bytes 147460
  16.5 100.8 %all-to-all-start = ((bf16[112,3,6144]{0,1,2:T(4,128)(2,1)}), bf16[112,3,6144]{0,1,2:T(4,128)(2,1)}, u32[]{:S(2)}, u32[]{:S(2)}) async-start(bf16[112,3,6144]{0,1,2:T(4,128)(2,1)} %bitcast.81), calls=%async_computation | async-start | bytes 12582912 | tf_op jit(solution)/shard_map/all_to_all | solution.py:67
  24.6 470.9 %reduce-scatter.2.cloned.1.call-start = ((), (), s32[]{:S(2)}) async-start(), calls=%async_computation.2 | async-start | bytes 24772608 | tf_op jit(solution)/shard_map/reduce_scatter | solution.py:79
  181.6 10.8 %copy-start.1 = (bf16[2,1344,6,128]{3,1,2,0:T(8,128)(2,1)S(1)}, bf16[2,1344,6,128]{3,1,2,0:T(8,128)(2,1)}, u32[]{:S(2)}) copy-start(bf16[2,1344,6,128]{3,1,2,0:T(8,128)(2,1)} %get-tuple-element.270) | copy-start | bytes 12386308 | tf_op jit(solution)/shard_map/while
  192.4 1.3 copy-start.2
  222.1 10.8 %copy-start.1 = (bf16[2,1344,6,128]{3,1,2,0:T(8,128)(2,1)S(1)}, bf16[2,1344,6,128]{3,1,2,0:T(8,128)(2,1)}, u32[]{:S(2)}) copy-start(bf16[2,1344,6,128]{3,1,2,0:T(8,128)(2,1)} %get-tuple-element.270) | copy-start | bytes 12386308 | tf_op jit(solution)/shard_map/while
  232.9 1.3 copy-start.2
  263.5 232.0 %copy-start.3 = (f32[1,112,6144]{2,1,0:T(8,128)S(1)}, f32[1,112,6144]{2,1,0:T(8,128)}, u32[]{:S(2)}) copy-start(f32[1,112,6144]{2,1,0:T(8,128)} %param.12) | copy-start | bytes 8257540
  498.8 34.7 %collective-permute-start = (f32[1,112,6144]{2,1,0:T(8,128)S(1)}, f32[1,112,6144]{2,1,0:T(8,128)S(1)}, u32[]{:S(2)}, u32[]{:S(2)}) collective-permute-start(f32[1,112,6144]{2,1,0:T(8,128)S(1)} %fusion.27), channel_id=1, source_target_pairs={{0,8},{8,16},{16,24},{24,32},{32,40},{40,48},{48,56},{56,64},{64,7... | collective-permute-start | bytes 8257544 | tf_op jit(solution)/shard_map/ppermute | solution.py:17
Sparse Core Ops, SparseCore 0:
  263.7 231.7 reduce-scatter.1
where the time goes:
time: 546 us; the launch traced here: 542 us
  waiting for transfers between devices  326 us (60%)
  local copies, waits for them, and re-layouts  81.2 us (15%)
  matrix products  67 us (12%)
  other arithmetic  45 us (8%)
  between operations  14.7 us (3%)
  starting transfers between devices  8.16 us (1%)
    reduce_scatter x1, waiting for transfers between devices, per_device(): lax.psum_scatter(jnp.dot(heads_all, out_proj[0], preferred_element_type=j...  232 us
    all_to_all x1, waiting for transfers between devices, per_device(): lax.all_to_all(qkv[0], 'sp', split_axis=2, concat_axis=0, tiled=True)  59 us
    ppermute x1, waiting for transfers between devices, passed_along(): lax.ppermute(shard, axis, [(i, (i + by) % devices) for i in range(devices)])  34.6 us
    reduce_max x4, other arithmetic, mix_video(): highest = jnp.max(scores, axis=2, keepdims=True)  23.2 us
    reduce_sum x2, other arithmetic, mix_video(): jnp.sum(raised, axis=2, keepdims=True)  21.6 us
    dot_general x2, matrix products, mix_video(): jnp.einsum('hqk,khe->qhe', weights, values_all, preferred_element_type=jn...  20.1 us
    dot_general x2, matrix products, far_scores(): jnp.einsum('qhe,khe->hqk', queries, cache_keys, preferred_element_type=jn...  18 us
    dot_general x1, matrix products, per_device(): jnp.dot(heads_all, out_proj[0], preferred_element_type=jnp.float32)  16.9 us
  transfers between devices with their start and end apart: 3, of which 3 were waited for; matrix products, arithmetic and copies ran while one was open for 6% of the time, Pallas kernels for 0%

commit v1 on v0

--- a/solution.py
+++ b/solution.py
@@ -76,12 +76,11 @@
     heads_all = lax.map(mix_one, (far_all, queries, own_keys, own_values, cache_values)).reshape(
         TOKS, local_width
     )
-    projected = lax.psum_scatter(
-        jnp.dot(heads_all, out_proj[0], preferred_element_type=jnp.float32),
-        "sp",
-        scatter_dimension=0,
-        tiled=True,
-    )
+    partial = jnp.dot(heads_all, out_proj[0], preferred_element_type=jnp.float32)
+    devices = lax.axis_size("sp")
+    shares = partial.astype(jnp.bfloat16).reshape(devices, own_rows, partial.shape[1])
+    shares = lax.all_to_all(shares, "sp", 0, 0, tiled=True)
+    projected = jnp.sum(shares.astype(jnp.float32), axis=0)
     device_place = lax.axis_index("sp")
     video_of = (device_place * own_rows + jnp.arange(own_rows, dtype=jnp.int32)) // SPAN
     picker = (video_of[:, None] == jnp.arange(VIDS, dtype=jnp.int32)[None, :]).astype(jnp.float32)

time: 546 us -> 469 us (0.86)
  waiting for transfers between devices: 326 us -> 254 us
  between operations: 14.7 us -> 1.37 us
  starting transfers between devices: 8.16 us -> 15.1 us
  other arithmetic: 45 us -> 51.5 us
    reduce_scatter x1 -> x0, waiting for transfers between devices: 232 us -> none  [per_device(): lax.psum_scatter(jnp.dot(heads_all, out_proj[0], preferred_element_type=j...]
    all_to_all x0 -> x1, waiting for transfers between devices: none -> 160 us  [per_device(): shares = lax.all_to_all(shares, 'sp', 0, 0, tiled=True)]
    all_to_all x0 -> x1, starting transfers between devices: none -> 6.91 us  [per_device(): shares = lax.all_to_all(shares, 'sp', 0, 0, tiled=True)]
    reduce_sum x0 -> x1, other arithmetic: none -> 6.42 us  [per_device(): projected = jnp.sum(shares.astype(jnp.float32), axis=0)]
  transfers between devices with their start and end apart: 3 -> 3, of which waited for: 3 -> 3; matrix products, arithmetic and copies ran while one was open for 6% -> 7% of each run, Pallas kernels for 0% -> 0%
where the time goes in v1:
time: 469 us; the launch traced here: 467 us
  waiting for transfers between devices  254 us (54%)
  local copies, waits for them, and re-layouts  81.3 us (17%)
  matrix products  63.6 us (14%)
  other arithmetic  51.5 us (11%)
  starting transfers between devices  15.1 us (3%)
    all_to_all x1, waiting for transfers between devices, per_device(): shares = lax.all_to_all(shares, 'sp', 0, 0, tiled=True)  160 us
    all_to_all x1, waiting for transfers between devices, per_device(): lax.all_to_all(qkv[0], 'sp', split_axis=2, concat_axis=0, tiled=True)  59.1 us
    ppermute x1, waiting for transfers between devices, passed_along(): lax.ppermute(shard, axis, [(i, (i + by) % devices) for i in range(devices)])  34.6 us
    reduce_max x4, other arithmetic, mix_video(): highest = jnp.max(scores, axis=2, keepdims=True)  23.2 us
    reduce_sum x2, other arithmetic, mix_video(): jnp.sum(raised, axis=2, keepdims=True)  21.6 us
    dot_general x2, matrix products, mix_video(): jnp.einsum('hqk,khe->qhe', weights, values_all, preferred_element_type=jn...  20.1 us
    dot_general x2, matrix products, far_scores(): jnp.einsum('qhe,khe->hqk', queries, cache_keys, preferred_element_type=jn...  18 us
    dot_general x1, matrix products, per_device(): jnp.dot(heads_all, out_proj[0], preferred_element_type=jnp.float32)  15.2 us
  transfers between devices with their start and end apart: 3, of which 3 were waited for; matrix products, arithmetic and copies ran while one was open for 7% of the time, Pallas kernels for 0%

profile of v1, /device:TPU:6, one launch (start us, length us, event | category | flops | bytes accessed | tf_op | source)
XLA Modules:
  0.0 466.9 jit_solution(14958061917673568924)
XLA Ops:
  0.0 10.0 %copy.53 = bf16[1,112,3,6144]{1,2,3,0:T(4,128)(2,1)} copy(bf16[1,112,3,6144]{3,1,2,0:T(8,128)(2,1)} %param.13) | data formatting | bytes 8257536 | tf_op args[1]
  10.0 8.1 %all-to-all-start = ((bf16[112,3,6144]{0,1,2:T(4,128)(2,1)}), bf16[112,3,6144]{0,1,2:T(4,128)(2,1)}, u32[]{:S(2)}, u32[]{:S(2)}) async-start(bf16[112,3,6144]{0,1,2:T(4,128)(2,1)} %bitcast.82), calls=%async_computation | async-start | bytes 12582912 | tf_op jit(solution)/shard_map/all_to_all | solution.py:67
  19.4 5.7 %fusion.30 = (bf16[1,1,2,1344,768]{4,3,2,1,0:T(8,128)(2,1)}, bf16[1,1,2,1344,768]{4,3,2,1,0:T(8,128)(2,1)}) fusion(bf16[1,2,2,1344,768]{4,3,2,1,0:T(8,128)(2,1)} %param.14), kind=kLoop, calls=%fused_computation.45 | loop fusion | bytes 16515072 | tf_op jit(solution)/shard_map/slice | solution.py:61
  25.1 6.4 %copy.58 = bf16[1,1,2,1344,768]{3,4,2,1,0:T(8,128)(2,1)} copy(bf16[1,1,2,1344,768]{4,3,2,1,0:T(8,128)(2,1)} %get-tuple-element.147) | data formatting | bytes 8257536 | tf_op jit(solution)/shard_map/slice | solution.py:61
  31.5 6.4 %copy.60 = bf16[2,1344,6,128]{3,1,2,0:T(8,128)(2,1)} copy(bf16[2,1344,6,128]{1,3,2,0:T(8,128)(2,1)} %bitcast.83) | data formatting | bytes 8257536 | tf_op jit(solution)/shard_map/while | solution.py:69
  38.0 6.4 %copy.52 = bf16[1,1,2,1344,768]{3,4,2,1,0:T(8,128)(2,1)} copy(bf16[1,1,2,1344,768]{4,3,2,1,0:T(8,128)(2,1)} %get-tuple-element.148) | data formatting | bytes 8257536 | tf_op jit(solution)/shard_map/slice | solution.py:62
  44.4 6.4 %copy.62 = bf16[2,1344,6,128]{3,1,2,0:T(8,128)(2,1)} copy(bf16[2,1344,6,128]{1,3,2,0:T(8,128)(2,1)} %bitcast.84) | data formatting | bytes 8257536 | tf_op jit(solution)/shard_map/while | solution.py:76
  50.8 0.7 dynamic-slice_bitcast_fusion.3
  51.5 0.2 select_reduce_fusion
  51.7 59.1 %all-to-all-done = bf16[112,3,6144]{0,1,2:T(4,128)(2,1)} async-done(((bf16[112,3,6144]{0,1,2:T(4,128)(2,1)}), bf16[112,3,6144]{0,1,2:T(4,128)(2,1)}, u32[]{:S(2)}, u32[]{:S(2)}) %all-to-all-start) | async-done | bytes 4128800 | tf_op jit(solution)/shard_map/all_to_all | solution.py:67
  110.8 10.0 %copy.68 = bf16[112,3,8,768]{3,0,2,1:T(8,128)(2,1)} copy(bf16[112,3,8,768]{0,1,3,2:T(4,128)(2,1)} %bitcast.14) | data formatting | bytes 8257536 | tf_op jit(solution)/shard_map/all_to_all | solution.py:67
  120.8 3.5 fusion.31
  124.3 2.5 reshape.36
  126.8 1.7 copy.59
  128.5 18.3 %while.20 = (s32[]{:T(128)}, f32[2,6,448,1344]{3,2,1,0:T(8,128)}, pred[3]{0:T(512)(128)(4,1)S(1)}, bf16[2,448,6,128]{3,1,2,0:T(8,128)(2,1)S(1)}, bf16[2,1344,6,128]{3,1,2,0:T(8,128)(2,1)}, /*index=5*/s32[]{:T(128)}) while((s32[]{:T(128)}, f32[2,6,448,1344]{3,2,1,0:T(8,128)}, pred[3]{0:T(512)(128)(4,1)S(1)}, ...), condition=%wide.region_2.3_spmd, body=%wide.region_1.2_spmd.sunk | while | flops 932069376 | bytes 17899016 | solution.py:69
  128.7 8.9 %bitcast_dynamic-update-slice_fusion.2 = f32[2,6,448,1344]{3,2,1,0:T(8,128)} fusion(f32[2,6,448,1344]{3,2,1,0:T(8,128)} %get-tuple-element.241, s32[]{:T(128)} %get-tuple-element.240, pred[1344]{0:T(1024)(128)(4,1)S(1)} %broadcast_in_dim.72, bf16[2,1344,6,128]{3,1,2,0:T(8,128)(2,1)} %get-tuple-element.250, ...), kind=kOutput, calls=%fused_computation.clone.1 | convolution fusion | flops 932069376 | bytes 17894912 | tf_op jit(solution)/shard_map/while/body/eval_jaxpr/qhe,khe->hqk/dot_general | solution.py:32
  137.8 9.0 %bitcast_dynamic-update-slice_fusion.2 = f32[2,6,448,1344]{3,2,1,0:T(8,128)} fusion(f32[2,6,448,1344]{3,2,1,0:T(8,128)} %get-tuple-element.241, s32[]{:T(128)} %get-tuple-element.240, pred[1344]{0:T(1024)(128)(4,1)S(1)} %broadcast_in_dim.72, bf16[2,1344,6,128]{3,1,2,0:T(8,128)(2,1)} %get-tuple-element.250, ...), kind=kOutput, calls=%fused_computation.clone.1 | convolution fusion | flops 932069376 | bytes 17894912 | tf_op jit(solution)/shard_map/while/body/eval_jaxpr/qhe,khe->hqk/dot_general | solution.py:32
  146.8 4.1 reshape.34
  151.0 2.8 copy.63
  153.8 2.5 reshape.35
  156.3 2.8 copy.65
  159.1 81.1 %while.21 = (s32[]{:T(128)}, bf16[2,448,768]{2,1,0:T(8,128)(2,1)}, bf16[2,1344,6,128]{3,1,2,0:T(8,128)(2,1)}, bf16[2,448,6,128]{3,1,2,0:T(8,128)(2,1)}, f32[2,6,...) while((s32[]{:T(128)}, bf16[2,448,768]{2,1,0:T(8,128)(2,1)}, ...), condition=%wide.region_7.8_spmd, body=%wide.region_3.7_spmd.sunk | while | flops 1586989824 | bytes 108822680 | solution.py:76
  159.1 4.4 fusion.42
  163.5 11.6 %dynamic-slice_reduce_fusion.2 = (f32[6,448]{1,0:T(8,128)S(1)}, f32[6,448,1344]{2,1,0:T(8,128)}) fusion(f32[2,6,448,1344]{3,2,1,0:T(8,128)} %get-tuple-element.272, s32[]{:T(128)} %get-tuple-element.260), kind=kLoop, calls=%fused_computation.9.clone.1 | loop fusion | flops 3609984 | bytes 28912132 | tf_op jit(solution)/shard_map/while/body/eval_jaxpr/reduce_max | solution.py:47
  175.1 10.8 %fusion.43 = f32[6,448]{1,0:T(8,128)S(1)} fusion(f32[6,448,448]{2,1,0:T(8,128)} %get-tuple-element.230, f32[6,448,1344]{2,1,0:T(8,128)} %get-tuple-element.231, f32[6,448]{1,0:T(8,128)S(1)} %reduce_max.27), kind=kLoop, calls=%fused_computation.11.clone.1 | loop fusion | flops 14448000 | bytes 19289088 | tf_op jit(solution)/shard_map/while/body/eval_jaxpr/reduce_sum | solution.py:49
  185.9 0.1 dynamic-slice_bitcast_fusion.7
  186.1 1.2 copy-done.2
  187.2 0.9 dynamic-slice_bitcast_fusion.6
  188.1 10.0 %fusion.44 = bf16[448,6,128]{2,0,1:T(8,128)(2,1)S(1)} fusion(bf16[448,6,128]{2,0,1:T(8,128)(2,1)} %dynamic-slice_bitcast_fusion.6, bf16[1344,6,128]{2,0,1:T(8,128)(2,1)S(1)} %dynamic-slice_bitcast_fusion.7, f32[6,448,448]{2,1,0:T(8,128)} %get-tuple-element.230, f32[6,448,1344]{2,1,0:T(8,128)} %get-tuple-element.231, f32[6,448]{1,0:T(8,128)S(1)} %fusion.43, ...), kind=kOutput, calls=%fused_computation.19.clone.1 | convolution fusion | flops 1258242048 | bytes 22729728 | tf_op jit(solution)/shard_map/while/body/eval_jaxpr/hqk,khe->qhe/dot_general | solution.py:51
  198.2 0.3 copy.79
  198.4 0.3 copy.80
  198.7 0.9 constant_dynamic-update-slice_fusion.2
  199.6 4.4 fusion.42
  204.0 11.6 %dynamic-slice_reduce_fusion.2 = (f32[6,448]{1,0:T(8,128)S(1)}, f32[6,448,1344]{2,1,0:T(8,128)}) fusion(f32[2,6,448,1344]{3,2,1,0:T(8,128)} %get-tuple-element.272, s32[]{:T(128)} %get-tuple-element.260), kind=kLoop, calls=%fused_computation.9.clone.1 | loop fusion | flops 3609984 | bytes 28912132 | tf_op jit(solution)/shard_map/while/body/eval_jaxpr/reduce_max | solution.py:47
  215.6 10.8 %fusion.43 = f32[6,448]{1,0:T(8,128)S(1)} fusion(f32[6,448,448]{2,1,0:T(8,128)} %get-tuple-element.230, f32[6,448,1344]{2,1,0:T(8,128)} %get-tuple-element.231, f32[6,448]{1,0:T(8,128)S(1)} %reduce_max.27), kind=kLoop, calls=%fused_computation.11.clone.1 | loop fusion | flops 14448000 | bytes 19289088 | tf_op jit(solution)/shard_map/while/body/eval_jaxpr/reduce_sum | solution.py:49
  226.6 1.2 copy-done.2
  227.8 0.9 dynamic-slice_bitcast_fusion.6
  228.6 10.0 %fusion.44 = bf16[448,6,128]{2,0,1:T(8,128)(2,1)S(1)} fusion(bf16[448,6,128]{2,0,1:T(8,128)(2,1)} %dynamic-slice_bitcast_fusion.6, bf16[1344,6,128]{2,0,1:T(8,128)(2,1)S(1)} %dynamic-slice_bitcast_fusion.7, f32[6,448,448]{2,1,0:T(8,128)} %get-tuple-element.230, f32[6,448,1344]{2,1,0:T(8,128)} %get-tuple-element.231, f32[6,448]{1,0:T(8,128)S(1)} %fusion.43, ...), kind=kOutput, calls=%fused_computation.19.clone.1 | convolution fusion | flops 1258242048 | bytes 22729728 | tf_op jit(solution)/shard_map/while/body/eval_jaxpr/hqk,khe->qhe/dot_general | solution.py:51
  238.7 0.3 copy.79
  239.0 0.3 copy.80
  239.2 0.9 constant_dynamic-update-slice_fusion.2
  240.1 15.2 %convolution_convert_fusion = bf16[896,6144]{1,0:T(8,128)(2,1)} fusion(bf16[896,768]{1,0:T(8,128)(2,1)} %bitcast.87, bf16[1,768,6144]{2,1,0:T(8,128)(2,1)} %param.15), kind=kOutput, calls=%fused_computation.30 | convolution fusion | flops 8461221888 | bytes 21823488 | tf_op jit(solution)/shard_map/dot_general | solution.py:79
  255.4 6.9 %all-to-all-start.1 = ((bf16[8,112,6144]{2,1,0:T(8,128)(2,1)}), bf16[8,112,6144]{2,1,0:T(8,128)(2,1)}, u32[]{:S(2)}, u32[]{:S(2)}) async-start(bf16[8,112,6144]{2,1,0:T(8,128)(2,1)} %bitcast.86), calls=%async_computation.1 | async-start | bytes 22020096 | tf_op jit(solution)/shard_map/all_to_all | solution.py:82
  262.3 160.4 %all-to-all-done.1 = bf16[8,112,6144]{2,1,0:T(8,128)(2,1)} async-done(((bf16[8,112,6144]{2,1,0:T(8,128)(2,1)}), bf16[8,112,6144]{2,1,0:T(8,128)(2,1)}, u32[]{:S(2)}, u32[]{:S(2)}) %all-to-all-start.1) | async-done | bytes 11010080 | tf_op jit(solution)/shard_map/all_to_all | solution.py:82
  422.7 6.4 %convert_reduce_fusion = f32[112,6144]{1,0:T(8,128)S(1)} fusion(bf16[8,112,6144]{2,1,0:T(8,128)(2,1)} %all-to-all-done.1), kind=kLoop, calls=%fused_computation.29 | loop fusion | flops 10321920 | bytes 13762560 | tf_op jit(solution)/shard_map/reduce_sum | solution.py:83
  429.1 1.6 fusion.26
  430.8 34.6 %collective-permute-done = f32[1,112,6144]{2,1,0:T(8,128)S(1)} collective-permute-done((f32[1,112,6144]{2,1,0:T(8,128)S(1)}, f32[1,112,6144]{2,1,0:T(8,128)S(1)}, u32[]{:S(2)}, u32[]{:S(2)}) %collective-permute-start) | collective-permute-done | bytes 2752544 | tf_op jit(solution)/shard_map/ppermute | solution.py:17
  465.4 1.5 copy.100
  (23 shorter events, 0.6 us)
Async XLA Ops:
  0.0 429.1 %copy-start = (f32[1,2,6144]{2,1,0:T(2,128)S(1)}, f32[1,2,6144]{2,1,0:T(2,128)}, u32[]{:S(2)}) copy-start(f32[1,2,6144]{2,1,0:T(2,128)} %param.16) | copy-start | bytes 147460
  10.0 100.8 %all-to-all-start = ((bf16[112,3,6144]{0,1,2:T(4,128)(2,1)}), bf16[112,3,6144]{0,1,2:T(4,128)(2,1)}, u32[]{:S(2)}, u32[]{:S(2)}) async-start(bf16[112,3,6144]{0,1,2:T(4,128)(2,1)} %bitcast.82), calls=%async_computation | async-start | bytes 12582912 | tf_op jit(solution)/shard_map/all_to_all | solution.py:67
  175.1 10.8 %copy-start.1 = (bf16[2,1344,6,128]{3,1,2,0:T(8,128)(2,1)S(1)}, bf16[2,1344,6,128]{3,1,2,0:T(8,128)(2,1)}, u32[]{:S(2)}) copy-start(bf16[2,1344,6,128]{3,1,2,0:T(8,128)(2,1)} %get-tuple-element.270) | copy-start | bytes 12386308 | tf_op jit(solution)/shard_map/while
  185.9 1.3 copy-start.2
  215.6 10.8 %copy-start.1 = (bf16[2,1344,6,128]{3,1,2,0:T(8,128)(2,1)S(1)}, bf16[2,1344,6,128]{3,1,2,0:T(8,128)(2,1)}, u32[]{:S(2)}) copy-start(bf16[2,1344,6,128]{3,1,2,0:T(8,128)(2,1)} %get-tuple-element.270) | copy-start | bytes 12386308 | tf_op jit(solution)/shard_map/while
  226.4 1.3 copy-start.2
  255.4 167.3 %all-to-all-start.1 = ((bf16[8,112,6144]{2,1,0:T(8,128)(2,1)}), bf16[8,112,6144]{2,1,0:T(8,128)(2,1)}, u32[]{:S(2)}, u32[]{:S(2)}) async-start(bf16[8,112,6144]{2,1,0:T(8,128)(2,1)} %bitcast.86), calls=%async_computation.1 | async-start | bytes 22020096 | tf_op jit(solution)/shard_map/all_to_all | solution.py:82
  262.3 166.8 %copy-start.3 = (f32[1,112,6144]{2,1,0:T(8,128)S(1)}, f32[1,112,6144]{2,1,0:T(8,128)}, u32[]{:S(2)}) copy-start(f32[1,112,6144]{2,1,0:T(8,128)} %param.12) | copy-start | bytes 8257540
  430.7 34.7 %collective-permute-start = (f32[1,112,6144]{2,1,0:T(8,128)S(1)}, f32[1,112,6144]{2,1,0:T(8,128)S(1)}, u32[]{:S(2)}, u32[]{:S(2)}) collective-permute-start(f32[1,112,6144]{2,1,0:T(8,128)S(1)} %fusion.26), channel_id=1, source_target_pairs={{0,8},{8,16},{16,24},{24,32},{32,40},{40,48},{48,56},{56,64},{64,7... | collective-permute-start | bytes 8257544 | tf_op jit(solution)/shard_map/ppermute | solution.py:17

commit v2 on v1

v2 whole, which is shorter than its diff:
```python
import jax
import jax.numpy as jnp
from jax import lax
from jax.experimental import pallas as pl
from jax.experimental.pallas import tpu as pltpu
from jax.sharding import PartitionSpec as P

HDIM = 128
SPAN = 448
NCHUNK = 40
SLOTS = 3
VIDS = 2
TOKS = 896
KEYS = 1344


def passed_along(shard, axis, by):
    devices = lax.axis_size(axis)
    return lax.ppermute(shard, axis, [(i, (i + by) % devices) for i in range(devices)])


def visible_slots(span_id, filled, span_mask):
    row_mask = lax.dynamic_index_in_dim(span_mask, span_id, 0, keepdims=False)
    slot_ids = jnp.arange(SLOTS, dtype=jnp.int32)
    wanted = span_id - 1 - slot_ids
    columns = jnp.arange(NCHUNK, dtype=jnp.int32)
    looked = jnp.sum(jnp.where(columns[None, :] == wanted[:, None], row_mask[None, :], 0), axis=1)
    return (slot_ids < filled) & (looked == 1)


def attend_kernel(bias_ref, q_ref, kn_ref, vn_ref, kc_ref, vc_ref, out_ref):
    score_scale = HDIM ** (-0.5)
    q = q_ref[...].reshape(SPAN, HDIM)
    kn = kn_ref[...].reshape(SPAN, HDIM)
    vn = vn_ref[...].reshape(SPAN, HDIM)
    kc = kc_ref[0, 0]
    vc = vc_ref[0, 0]
    contract = (((1,), (1,)), ((), ()))
    far = lax.dot_general(q, kc, contract, preferred_element_type=jnp.float32) * score_scale
    far = far + bias_ref[...]
    near = lax.dot_general(q, kn, contract, preferred_element_type=jnp.float32) * score_scale
    highest = jnp.maximum(jnp.max(far, axis=1, keepdims=True), jnp.max(near, axis=1, keepdims=True))
    far_raised = jnp.exp(far - highest)
    near_raised = jnp.exp(near - highest)
    total = jnp.sum(far_raised, axis=1, keepdims=True) + jnp.sum(near_raised, axis=1, keepdims=True)
    far_w = (far_raised / total).astype(jnp.bfloat16)
    near_w = (near_raised / total).astype(jnp.bfloat16)
    mixed = jnp.dot(far_w, vc, preferred_element_type=jnp.float32) + jnp.dot(
        near_w, vn, preferred_element_type=jnp.float32
    )
    out_ref[...] = mixed.astype(out_ref.dtype)


def attend_all(key_bias, spread, cache_kv, local_heads):
    groups = spread.shape[0]
    per_video = groups // VIDS
    rows = spread.shape[1]
    width = local_heads * HDIM

    def own_spec(part):
        return pl.BlockSpec((per_video, rows, HDIM), lambda b, h: (b, 0, part * local_heads + h))

    return pl.pallas_call(
        attend_kernel,
        grid=(VIDS, local_heads),
        in_specs=[
            pl.BlockSpec((1, KEYS), lambda b, h: (0, 0)),
            own_spec(0),
            own_spec(1),
            own_spec(2),
            pl.BlockSpec((1, 1, KEYS, HDIM), lambda b, h: (0, b, 0, h)),
            pl.BlockSpec((1, 1, KEYS, HDIM), lambda b, h: (1, b, 0, h)),
        ],
        out_specs=pl.BlockSpec((SPAN, HDIM), lambda b, h: (b, h)),
        out_shape=jax.ShapeDtypeStruct((TOKS, width), jnp.bfloat16),
    )(key_bias, spread, spread, spread, cache_kv, cache_kv)


def per_device(resid, qkv, cache_kv, out_proj, gate, span_ids, cache_counts, span_mask):
    own_rows = resid.shape[1]
    local_width = cache_kv.shape[4]
    local_heads = local_width // HDIM
    devices = lax.axis_size("sp")
    filled = cache_counts[0]
    live_slots = visible_slots(span_ids[0], filled, span_mask)
    key_bias = jnp.repeat(jnp.where(live_slots, 0.0, -jnp.inf).astype(jnp.float32), SPAN)[None, :]

    grouped = qkv[0].reshape(own_rows, 3, devices, local_width).transpose(2, 0, 1, 3)
    spread = lax.all_to_all(grouped, "sp", 0, 0, tiled=True)
    spread = spread.reshape(devices, own_rows, 3 * local_width)
    heads_all = attend_all(key_bias, spread, cache_kv[0], local_heads)

    partial = jnp.dot(heads_all, out_proj[0], preferred_element_type=jnp.float32)
    shares = partial.astype(jnp.bfloat16).reshape(devices, own_rows, partial.shape[1])
    shares = lax.all_to_all(shares, "sp", 0, 0, tiled=True)
    projected = jnp.sum(shares.astype(jnp.float32), axis=0)
    device_place = lax.axis_index("sp")
    video_of = (device_place * own_rows + jnp.arange(own_rows, dtype=jnp.int32)) // SPAN
    picker = (video_of[:, None] == jnp.arange(VIDS, dtype=jnp.int32)[None, :]).astype(jnp.float32)
    gains = jnp.dot(picker, gate[0], precision=lax.Precision.HIGHEST)
    layer_out = resid[0] + gains * projected
    return passed_along(layer_out[None], "section", 1)


def solution(mesh):
    in_specs = (
        P("section", "sp", None),
        P("section", "sp", None, None),
        P("section", None, None, None, "sp"),
        P("section", "sp", None),
        P("section", None, None),
        P("section"),
        P("section"),
        P(),
    )
    out_specs = P("section", "sp", None)
    return jax.shard_map(
        per_device, mesh=mesh, in_specs=in_specs, out_specs=out_specs, check_vma=False
    )
```

time: 469 us -> 345 us (0.74)
  local copies, waits for them, and re-layouts: 81.3 us -> 22.1 us
  matrix products: 63.6 us -> 16.8 us
  other arithmetic: 51.5 us -> 6.63 us
  Pallas kernels: 0 us -> 30 us
    dot_general x6 -> x0, matrix products: 46.8 us -> none  [the longest x2 20.1 us: mix_video(): jnp.einsum('hqk,khe->qhe', weights, values_all, preferred_element_type=jn...]
    pallas_call x0 -> x1, Pallas kernels: none -> 30 us  [attend_all(): pl.pallas_call(attend_kernel, grid=(VIDS, local_heads), in_specs=[pl.Bloc...]
    reduce_max x4 -> x0, other arithmetic: 23.2 us -> none  [mix_video(): highest = jnp.max(scores, axis=2, keepdims=True)]
    while x13 -> x0, local copies, waits for them, and re-layouts: 22.5 us -> none  [the longest x3 12.1 us: per_device(): lax.map(mix_one, (far_all, queries, own_keys, own_values, cache_values))]
    slice x4 -> x0, local copies, waits for them, and re-layouts: 22.1 us -> none  [the longest x2 12.1 us: per_device(): cache_keys = cache_kv[0, 0].reshape(VIDS, KEYS, local_heads, HDIM)]
    reduce_sum x2 -> x0, other arithmetic: 21.6 us -> none  [mix_video(): jnp.sum(raised, axis=2, keepdims=True)]
    another operation x3 -> x1, local copies, waits for them, and re-layouts: 9.1 us -> 0.68 us  [per_device(): jnp.repeat(jnp.where(live_slots, 0.0, -jnp.inf).astype(jnp.float32), SPAN)]
    unnamed x6, local copies, waits for them, and re-layouts: 11.6 us -> 4.93 us
  transfers between devices with their start and end apart: 3 -> 3, of which waited for: 3 -> 3; matrix products, arithmetic and copies ran while one was open for 7% -> 0% of each run, Pallas kernels for 0% -> 0%
where the time goes in v2:
time: 345 us; the launch traced here: 344 us
  waiting for transfers between devices  252 us (73%)
  Pallas kernels  30 us (9%)
  local copies, waits for them, and re-layouts  22.1 us (6%)
  matrix products  16.8 us (5%)
  starting transfers between devices  15.1 us (4%)
  other arithmetic  6.63 us (2%)
    all_to_all x1, waiting for transfers between devices, per_device(): shares = lax.all_to_all(shares, 'sp', 0, 0, tiled=True)  160 us
    all_to_all x1, waiting for transfers between devices, per_device(): spread = lax.all_to_all(grouped, 'sp', 0, 0, tiled=True)  57.3 us
    ppermute x1, waiting for transfers between devices, passed_along(): lax.ppermute(shard, axis, [(i, (i + by) % devices) for i in range(devices)])  34.6 us
    pallas_call x1, Pallas kernels, attend_all(): pl.pallas_call(attend_kernel, grid=(VIDS, local_heads), in_specs=[pl.Bloc...  30 us
    dot_general x1, matrix products, per_device(): jnp.dot(heads_all, out_proj[0], preferred_element_type=jnp.float32)  15.2 us
    all_to_all x1, starting transfers between devices, per_device(): spread = lax.all_to_all(grouped, 'sp', 0, 0, tiled=True)  8.09 us
    all_to_all x1, starting transfers between devices, per_device(): shares = lax.all_to_all(shares, 'sp', 0, 0, tiled=True)  6.91 us
  transfers between devices with their start and end apart: 3, of which 3 were waited for; matrix products, arithmetic and copies ran while one was open for 0% of the time, Pallas kernels for 0%

profile of v2, /device:TPU:6, one launch (start us, length us, event | category | flops | bytes accessed | tf_op | source)
XLA Modules:
  0.0 344.2 jit_solution(3029470605188074354)
XLA Ops:
  0.0 0.0 copy-start
  0.0 3.4 copy.28
  3.4 2.7 copy.23
  6.1 8.1 %all-to-all-start = ((bf16[8,112,3,768]{3,1,2,0:T(8,128)(2,1)}), bf16[8,112,3,768]{3,1,2,0:T(8,128)(2,1)}, u32[]{:S(2)}, u32[]{:S(2)}) async-start(bf16[8,112,3,768]{3,1,2,0:T(8,128)(2,1)} %copy.23), calls=%async_computation | async-start | bytes 8257536 | tf_op jit(solution)/shard_map/all_to_all | solution.py:89
  15.5 0.7 dynamic-slice_bitcast_fusion
  16.2 0.2 select_reduce_fusion
  16.4 0.1 broadcast_in_dim.38
  16.5 0.7 broadcast_in_dim_reshape.3.bias_ref
  17.2 57.3 %all-to-all-done = bf16[8,112,3,768]{3,1,2,0:T(8,128)(2,1)} async-done(((bf16[8,112,3,768]{3,1,2,0:T(8,128)(2,1)}), bf16[8,112,3,768]{3,1,2,0:T(8,128)(2,1)}, u32[]{:S(2)}, u32[]{:S(2)}) %all-to-all-start) | async-done | bytes 4128800 | tf_op jit(solution)/shard_map/all_to_all | solution.py:89
  74.5 6.5 %copy.24 = bf16[8,112,3,768]{1,3,2,0:T(8,128)(2,1)} copy(bf16[8,112,3,768]{3,1,2,0:T(8,128)(2,1)} %all-to-all-done) | data formatting | bytes 8257536 | tf_op jit(solution)/shard_map/all_to_all | solution.py:89
  80.9 6.5 %copy.25.q_ref.kn_ref.vn_ref = bf16[8,112,2304]{2,1,0:T(8,128)(2,1)} copy(bf16[8,112,2304]{1,2,0:T(8,128)(2,1)} %bitcast.34) | data formatting | bytes 8257536 | tf_op jit(solution)/shard_map/reshape | solution.py:90
  87.4 30.0 %shard_map.82 = bf16[896,768]{1,0:T(8,128)(2,1)} custom-call(f32[1,1344]{1,0:T(1,128)} %broadcast_in_dim_reshape.3.bias_ref, bf16[8,112,2304]{2,1,0:T(8,128)(2,1)} %copy.25.q_ref.kn_ref.vn_ref, bf16[8,112,2304]{2,1,0:T(8,128)(2,1)} %copy.25.q_ref.kn_ref.vn_ref, bf16[8,112,2304]{2,1,0:T(8,128)(2,1)} %copy.25.q_ref.kn_ref.vn_ref, ...), custom_call_target="tpu_custom_call" | custom-call | tf_op jit(solution)/shard_map/pallas_call | solution.py:63
  117.4 15.2 %convolution_convert_fusion = bf16[896,6144]{1,0:T(8,128)(2,1)} fusion(bf16[896,768]{1,0:T(8,128)(2,1)} %shard_map.82, bf16[1,768,6144]{2,1,0:T(8,128)(2,1)} %param.11), kind=kOutput, calls=%fused_computation.1 | convolution fusion | flops 8461221888 | bytes 21823488 | tf_op jit(solution)/shard_map/dot_general | solution.py:93
  132.6 6.9 %all-to-all-start.1 = ((bf16[8,112,6144]{2,1,0:T(8,128)(2,1)}), bf16[8,112,6144]{2,1,0:T(8,128)(2,1)}, u32[]{:S(2)}, u32[]{:S(2)}) async-start(bf16[8,112,6144]{2,1,0:T(8,128)(2,1)} %bitcast.36), calls=%async_computation.1 | async-start | bytes 22020096 | tf_op jit(solution)/shard_map/all_to_all | solution.py:95
  139.5 0.0 copy-start.1
  139.5 160.4 %all-to-all-done.1 = bf16[8,112,6144]{2,1,0:T(8,128)(2,1)} async-done(((bf16[8,112,6144]{2,1,0:T(8,128)(2,1)}), bf16[8,112,6144]{2,1,0:T(8,128)(2,1)}, u32[]{:S(2)}, u32[]{:S(2)}) %all-to-all-start.1) | async-done | bytes 11010080 | tf_op jit(solution)/shard_map/all_to_all | solution.py:95
  299.9 6.4 %convert_reduce_fusion = f32[112,6144]{1,0:T(8,128)S(1)} fusion(bf16[8,112,6144]{2,1,0:T(8,128)(2,1)} %all-to-all-done.1), kind=kLoop, calls=%fused_computation | loop fusion | flops 10321920 | bytes 13762560 | tf_op jit(solution)/shard_map/reduce_sum | solution.py:96
  306.4 0.0 copy-done
  306.4 0.0 copy-done.1
  306.4 1.6 fusion.2
  308.0 0.1 collective-permute-start
  308.1 34.6 %collective-permute-done = f32[1,112,6144]{2,1,0:T(8,128)S(1)} collective-permute-done((f32[1,112,6144]{2,1,0:T(8,128)S(1)}, f32[1,112,6144]{2,1,0:T(8,128)S(1)}, u32[]{:S(2)}, u32[]{:S(2)}) %collective-permute-start) | collective-permute-done | bytes 2752544 | tf_op jit(solution)/shard_map/ppermute | solution.py:19
  342.6 1.5 copy.32
  (3 shorter events, 0.0 us)
Async XLA Ops:
  0.0 306.4 %copy-start = (f32[1,2,6144]{2,1,0:T(2,128)S(1)}, f32[1,2,6144]{2,1,0:T(2,128)}, u32[]{:S(2)}) copy-start(f32[1,2,6144]{2,1,0:T(2,128)} %param.12) | copy-start | bytes 147460
  6.1 68.3 %all-to-all-start = ((bf16[8,112,3,768]{3,1,2,0:T(8,128)(2,1)}), bf16[8,112,3,768]{3,1,2,0:T(8,128)(2,1)}, u32[]{:S(2)}, u32[]{:S(2)}) async-start(bf16[8,112,3,768]{3,1,2,0:T(8,128)(2,1)} %copy.23), calls=%async_computation | async-start | bytes 8257536 | tf_op jit(solution)/shard_map/all_to_all | solution.py:89
  132.6 167.3 %all-to-all-start.1 = ((bf16[8,112,6144]{2,1,0:T(8,128)(2,1)}), bf16[8,112,6144]{2,1,0:T(8,128)(2,1)}, u32[]{:S(2)}, u32[]{:S(2)}) async-start(bf16[8,112,6144]{2,1,0:T(8,128)(2,1)} %bitcast.36), calls=%async_computation.1 | async-start | bytes 22020096 | tf_op jit(solution)/shard_map/all_to_all | solution.py:95
  139.5 166.8 %copy-start.1 = (f32[1,112,6144]{2,1,0:T(8,128)S(1)}, f32[1,112,6144]{2,1,0:T(8,128)}, u32[]{:S(2)}) copy-start(f32[1,112,6144]{2,1,0:T(8,128)} %param.8) | copy-start | bytes 8257540
  308.0 34.7 %collective-permute-start = (f32[1,112,6144]{2,1,0:T(8,128)S(1)}, f32[1,112,6144]{2,1,0:T(8,128)S(1)}, u32[]{:S(2)}, u32[]{:S(2)}) collective-permute-start(f32[1,112,6144]{2,1,0:T(8,128)S(1)} %fusion.2), channel_id=1, source_target_pairs={{0,8},{8,16},{16,24},{24,32},{32,40},{40,48},{48,56},{56,64},{64,7... | collective-permute-start | bytes 8257544 | tf_op jit(solution)/shard_map/ppermute | solution.py:19

commit v3 on v2

--- a/solution.py
+++ b/solution.py
@@ -90,16 +90,23 @@
     spread = spread.reshape(devices, own_rows, 3 * local_width)
     heads_all = attend_all(key_bias, spread, cache_kv[0], local_heads)
 
-    partial = jnp.dot(heads_all, out_proj[0], preferred_element_type=jnp.float32)
-    shares = partial.astype(jnp.bfloat16).reshape(devices, own_rows, partial.shape[1])
-    shares = lax.all_to_all(shares, "sp", 0, 0, tiled=True)
-    projected = jnp.sum(shares.astype(jnp.float32), axis=0)
     device_place = lax.axis_index("sp")
     video_of = (device_place * own_rows + jnp.arange(own_rows, dtype=jnp.int32)) // SPAN
     picker = (video_of[:, None] == jnp.arange(VIDS, dtype=jnp.int32)[None, :]).astype(jnp.float32)
     gains = jnp.dot(picker, gate[0], precision=lax.Precision.HIGHEST)
-    layer_out = resid[0] + gains * projected
-    return passed_along(layer_out[None], "section", 1)
+    width = out_proj.shape[2]
+    pieces = 3
+    step = width // pieces
+    outs = []
+    for c in range(pieces):
+        cols = slice(c * step, (c + 1) * step)
+        partial = jnp.dot(heads_all, out_proj[0, :, cols], preferred_element_type=jnp.float32)
+        shares = partial.astype(jnp.bfloat16).reshape(devices, own_rows, step)
+        shares = lax.all_to_all(shares, "sp", 0, 0, tiled=True)
+        projected = jnp.sum(shares.astype(jnp.float32), axis=0)
+        layer_out = resid[0, :, cols] + gains[:, cols] * projected
+        outs.append(passed_along(layer_out, "section", 1))
+    return jnp.concatenate(outs, axis=1)[None]
 
 
 def solution(mesh):

time: 345 us -> 324 us (0.939)
  waiting for transfers between devices: 252 us -> 206 us
  starting transfers between devices: 15.1 us -> 30.1 us
  other arithmetic: 6.63 us -> 13.1 us
  matrix products: 16.8 us -> 21.1 us
    all_to_all x1 -> x3, waiting for transfers between devices: 160 us -> 115 us  [per_device(): shares = lax.all_to_all(shares, 'sp', 0, 0, tiled=True)]
    all_to_all x1 -> x3, starting transfers between devices: 6.91 us -> 20.9 us  [per_device(): shares = lax.all_to_all(shares, 'sp', 0, 0, tiled=True)]
    dot_general x1 -> x3, matrix products: 15.2 us -> 19.8 us  [per_device(): jnp.dot(heads_all, out_proj[0, :, cols], preferred_element_type=jnp.float32)]
    reduce_sum x1 -> x3, other arithmetic: 6.42 us -> 10.4 us  [per_device(): projected = jnp.sum(shares.astype(jnp.float32), axis=0)]
    ppermute x1 -> x3, waiting for transfers between devices: 34.6 us -> 33.5 us  [passed_along(): lax.ppermute(shard, axis, [(i, (i + by) % devices) for i in range(devices)])]
  transfers between devices with their start and end apart: 3 -> 7, of which waited for: 3 -> 7; matrix products, arithmetic and copies ran while one was open for 0% -> 7% of each run, Pallas kernels for 0% -> 0%
where the time goes in v3:
time: 324 us; the launch traced here: 323 us
  waiting for transfers between devices  206 us (64%)
  starting transfers between devices  30.1 us (9%)
  Pallas kernels  30 us (9%)
  local copies, waits for them, and re-layouts  21.1 us (7%)
  matrix products  21.1 us (7%)
  other arithmetic  13.1 us (4%)
    all_to_all x3, waiting for transfers between devices, per_device(): shares = lax.all_to_all(shares, 'sp', 0, 0, tiled=True)  115 us
    all_to_all x1, waiting for transfers between devices, per_device(): spread = lax.all_to_all(grouped, 'sp', 0, 0, tiled=True)  57.3 us
    ppermute x3, waiting for transfers between devices, passed_along(): lax.ppermute(shard, axis, [(i, (i + by) % devices) for i in range(devices)])  33.5 us
    pallas_call x1, Pallas kernels, attend_all(): pl.pallas_call(attend_kernel, grid=(VIDS, local_heads), in_specs=[pl.Bloc...  30 us
    all_to_all x3, starting transfers between devices, per_device(): shares = lax.all_to_all(shares, 'sp', 0, 0, tiled=True)  20.9 us
    dot_general x3, matrix products, per_device(): jnp.dot(heads_all, out_proj[0, :, cols], preferred_element_type=jnp.float32)  19.8 us
    reduce_sum x3, other arithmetic, per_device(): projected = jnp.sum(shares.astype(jnp.float32), axis=0)  10.4 us
    all_to_all x1, starting transfers between devices, per_device(): spread = lax.all_to_all(grouped, 'sp', 0, 0, tiled=True)  8.09 us
  transfers between devices with their start and end apart: 7, of which 7 were waited for; matrix products, arithmetic and copies ran while one was open for 7% of the time, Pallas kernels for 0%

profile of v3, /device:TPU:6, one launch (start us, length us, event | category | flops | bytes accessed | tf_op | source)
XLA Modules:
  0.0 323.0 jit_solution(803686494691041001)
XLA Ops:
  0.0 0.0 copy-start
  0.0 3.4 %copy.28 = bf16[42,8,8,768]{3,2,1,0:T(8,128)(2,1)S(1)} copy(bf16[42,8,8,768]{3,1,2,0:T(8,128)(2,1)} %bitcast.50) | data formatting | bytes 8257536
  3.4 2.7 copy.23
  6.1 8.1 %all-to-all-start = ((bf16[8,112,3,768]{3,1,2,0:T(8,128)(2,1)}), bf16[8,112,3,768]{3,1,2,0:T(8,128)(2,1)}, u32[]{:S(2)}, u32[]{:S(2)}) async-start(bf16[8,112,3,768]{3,1,2,0:T(8,128)(2,1)} %copy.23), calls=%async_computation | async-start | bytes 8257536 | tf_op jit(solution)/shard_map/all_to_all | solution.py:89
  15.5 0.7 dynamic-slice_bitcast_fusion
  16.2 0.2 select_reduce_fusion
  16.4 0.1 broadcast_in_dim.38
  16.5 0.7 broadcast_in_dim_reshape.3.bias_ref
  17.2 57.3 %all-to-all-done = bf16[8,112,3,768]{3,1,2,0:T(8,128)(2,1)} async-done(((bf16[8,112,3,768]{3,1,2,0:T(8,128)(2,1)}), bf16[8,112,3,768]{3,1,2,0:T(8,128)(2,1)}, u32[]{:S(2)}, u32[]{:S(2)}) %all-to-all-start) | async-done | bytes 4128800 | tf_op jit(solution)/shard_map/all_to_all | solution.py:89
  74.5 6.5 %copy.24 = bf16[8,112,3,768]{1,3,2,0:T(8,128)(2,1)} copy(bf16[8,112,3,768]{3,1,2,0:T(8,128)(2,1)} %all-to-all-done) | data formatting | bytes 8257536 | tf_op jit(solution)/shard_map/all_to_all | solution.py:89
  80.9 6.6 %copy.25.q_ref.kn_ref.vn_ref = bf16[8,112,2304]{2,1,0:T(8,128)(2,1)} copy(bf16[8,112,2304]{1,2,0:T(8,128)(2,1)} %bitcast.48) | data formatting | bytes 8257536 | tf_op jit(solution)/shard_map/reshape | solution.py:90
  87.5 30.0 %shard_map.82 = bf16[896,768]{1,0:T(8,128)(2,1)} custom-call(f32[1,1344]{1,0:T(1,128)} %broadcast_in_dim_reshape.3.bias_ref, bf16[8,112,2304]{2,1,0:T(8,128)(2,1)} %copy.25.q_ref.kn_ref.vn_ref, bf16[8,112,2304]{2,1,0:T(8,128)(2,1)} %copy.25.q_ref.kn_ref.vn_ref, bf16[8,112,2304]{2,1,0:T(8,128)(2,1)} %copy.25.q_ref.kn_ref.vn_ref, ...), custom_call_target="tpu_custom_call" | custom-call | tf_op jit(solution)/shard_map/pallas_call | solution.py:63
  117.5 7.2 %convolution_convert_fusion = bf16[896,2048]{1,0:T(8,128)(2,1)} fusion(bf16[896,768]{1,0:T(8,128)(2,1)} %shard_map.82, bf16[1,768,6144]{2,1,0:T(8,128)(2,1)} %param.11), kind=kOutput, calls=%fused_computation.3 | convolution fusion | flops 2820407296 | bytes 8192000 | tf_op jit(solution)/shard_map/dot_general | solution.py:103
  124.7 0.0 copy-start.4
  124.7 7.0 %all-to-all-start.3 = ((bf16[8,112,2048]{2,1,0:T(8,128)(2,1)}), bf16[8,112,2048]{2,1,0:T(8,128)(2,1)}, u32[]{:S(2)}, u32[]{:S(2)}) async-start(bf16[8,112,2048]{2,1,0:T(8,128)(2,1)} %bitcast.53), calls=%async_computation.3 | async-start | bytes 7340032 | tf_op jit(solution)/shard_map/all_to_all | solution.py:105
  131.7 0.0 copy-done.4
  131.7 6.3 %convolution_convert_fusion.1 = bf16[896,2048]{1,0:T(8,128)(2,1)} fusion(bf16[896,768]{1,0:T(8,128)(2,1)S(1)} %copy-done.4, bf16[1,768,6144]{2,1,0:T(8,128)(2,1)} %param.11), kind=kOutput, calls=%fused_computation.4 | convolution fusion | flops 2820407296 | bytes 8192000 | tf_op jit(solution)/shard_map/dot_general | solution.py:103
  138.1 41.6 %all-to-all-done.3 = bf16[8,112,2048]{2,1,0:T(8,128)(2,1)} async-done(((bf16[8,112,2048]{2,1,0:T(8,128)(2,1)}), bf16[8,112,2048]{2,1,0:T(8,128)(2,1)}, u32[]{:S(2)}, u32[]{:S(2)}) %all-to-all-start.3) | async-done | bytes 3670048 | tf_op jit(solution)/shard_map/all_to_all | solution.py:105
  179.6 6.9 %all-to-all-start.2 = ((bf16[8,112,2048]{2,1,0:T(8,128)(2,1)}), bf16[8,112,2048]{2,1,0:T(8,128)(2,1)}, u32[]{:S(2)}, u32[]{:S(2)}) async-start(bf16[8,112,2048]{2,1,0:T(8,128)(2,1)} %bitcast.52), calls=%async_computation.2 | async-start | bytes 7340032 | tf_op jit(solution)/shard_map/all_to_all | solution.py:105
  186.5 6.3 %convolution_convert_fusion.2 = bf16[896,2048]{1,0:T(8,128)(2,1)} fusion(bf16[896,768]{1,0:T(8,128)(2,1)S(1)} %copy-done.4, bf16[1,768,6144]{2,1,0:T(8,128)(2,1)} %param.11), kind=kOutput, calls=%fused_computation.5 | convolution fusion | flops 2820407296 | bytes 8192000 | tf_op jit(solution)/shard_map/dot_general | solution.py:103
  192.9 35.7 %all-to-all-done.2 = bf16[8,112,2048]{2,1,0:T(8,128)(2,1)} async-done(((bf16[8,112,2048]{2,1,0:T(8,128)(2,1)}), bf16[8,112,2048]{2,1,0:T(8,128)(2,1)}, u32[]{:S(2)}, u32[]{:S(2)}) %all-to-all-start.2) | async-done | bytes 3670048 | tf_op jit(solution)/shard_map/all_to_all | solution.py:105
  228.6 6.9 %all-to-all-start.1 = ((bf16[8,112,2048]{2,1,0:T(8,128)(2,1)}), bf16[8,112,2048]{2,1,0:T(8,128)(2,1)}, u32[]{:S(2)}, u32[]{:S(2)}) async-start(bf16[8,112,2048]{2,1,0:T(8,128)(2,1)} %bitcast.51), calls=%async_computation.1 | async-start | bytes 7340032 | tf_op jit(solution)/shard_map/all_to_all | solution.py:105
  235.6 0.0 copy-done
  235.6 1.3 fusion.9
  236.8 3.7 %convert_reduce_fusion = f32[112,2048]{1,0:T(8,128)} fusion(bf16[8,112,2048]{2,1,0:T(8,128)(2,1)} %all-to-all-done.3), kind=kLoop, calls=%fused_computation | loop fusion | flops 3440640 | bytes 4587520 | tf_op jit(solution)/shard_map/reduce_sum | solution.py:106
  240.5 3.7 %convert_reduce_fusion.1 = f32[112,2048]{1,0:T(8,128)} fusion(bf16[8,112,2048]{2,1,0:T(8,128)(2,1)} %all-to-all-done.2), kind=kLoop, calls=%fused_computation.1 | loop fusion | flops 3440640 | bytes 4587520 | tf_op jit(solution)/shard_map/reduce_sum | solution.py:106
  244.2 38.1 %all-to-all-done.1 = bf16[8,112,2048]{2,1,0:T(8,128)(2,1)} async-done(((bf16[8,112,2048]{2,1,0:T(8,128)(2,1)}), bf16[8,112,2048]{2,1,0:T(8,128)(2,1)}, u32[]{:S(2)}, u32[]{:S(2)}) %all-to-all-start.1) | async-done | bytes 3670048 | tf_op jit(solution)/shard_map/all_to_all | solution.py:105
  282.3 0.0 copy-start.1
  282.3 0.0 copy-start.2
  282.3 0.0 copy-start.3
  282.3 3.0 convert_reduce_fusion.2
  285.3 0.0 copy-done.1
  285.3 0.0 copy-done.2
  285.3 0.4 copy-done.3
  285.8 0.8 fusion.8
  286.6 0.1 collective-permute-start
  286.7 1.0 collective-permute-start.1
  287.7 0.1 collective-permute-start.2
  287.8 13.8 %collective-permute-done = f32[112,2048]{1,0:T(8,128)S(1)} collective-permute-done((f32[112,2048]{1,0:T(8,128)S(1)}, f32[112,2048]{1,0:T(8,128)S(1)}, u32[]{:S(2)}, u32[]{:S(2)}) %collective-permute-start) | collective-permute-done | bytes 917536 | tf_op jit(solution)/shard_map/ppermute | solution.py:19
  301.6 9.8 %collective-permute-done.1 = f32[112,2048]{1,0:T(8,128)S(1)} collective-permute-done((f32[112,2048]{1,0:T(8,128)S(1)}, f32[112,2048]{1,0:T(8,128)S(1)}, u32[]{:S(2)}, u32[]{:S(2)}) %collective-permute-start.1) | collective-permute-done | bytes 917536 | tf_op jit(solution)/shard_map/ppermute | solution.py:19
  311.4 9.8 %collective-permute-done.2 = f32[112,2048]{1,0:T(8,128)S(1)} collective-permute-done((f32[112,2048]{1,0:T(8,128)S(1)}, f32[112,2048]{1,0:T(8,128)S(1)}, u32[]{:S(2)}, u32[]{:S(2)}) %collective-permute-start.2) | collective-permute-done | bytes 917536 | tf_op jit(solution)/shard_map/ppermute | solution.py:19
  321.2 1.7 maximum_bitcast_fusion
  (3 shorter events, 0.0 us)
Async XLA Ops:
  0.0 235.6 %copy-start = (f32[1,2,6144]{2,1,0:T(2,128)S(1)}, f32[1,2,6144]{2,1,0:T(2,128)}, u32[]{:S(2)}) copy-start(f32[1,2,6144]{2,1,0:T(2,128)} %param.12) | copy-start | bytes 147460
  6.1 68.3 %all-to-all-start = ((bf16[8,112,3,768]{3,1,2,0:T(8,128)(2,1)}), bf16[8,112,3,768]{3,1,2,0:T(8,128)(2,1)}, u32[]{:S(2)}, u32[]{:S(2)}) async-start(bf16[8,112,3,768]{3,1,2,0:T(8,128)(2,1)} %copy.23), calls=%async_computation | async-start | bytes 8257536 | tf_op jit(solution)/shard_map/all_to_all | solution.py:89
  124.7 7.1 %copy-start.4 = (bf16[896,768]{1,0:T(8,128)(2,1)S(1)}, bf16[896,768]{1,0:T(8,128)(2,1)}, u32[]{:S(2)}) copy-start(bf16[896,768]{1,0:T(8,128)(2,1)} %shard_map.82) | copy-start | bytes 4128772
  124.7 55.0 %all-to-all-start.3 = ((bf16[8,112,2048]{2,1,0:T(8,128)(2,1)}), bf16[8,112,2048]{2,1,0:T(8,128)(2,1)}, u32[]{:S(2)}, u32[]{:S(2)}) async-start(bf16[8,112,2048]{2,1,0:T(8,128)(2,1)} %bitcast.53), calls=%async_computation.3 | async-start | bytes 7340032 | tf_op jit(solution)/shard_map/all_to_all | solution.py:105
  179.6 49.0 %all-to-all-start.2 = ((bf16[8,112,2048]{2,1,0:T(8,128)(2,1)}), bf16[8,112,2048]{2,1,0:T(8,128)(2,1)}, u32[]{:S(2)}, u32[]{:S(2)}) async-start(bf16[8,112,2048]{2,1,0:T(8,128)(2,1)} %bitcast.52), calls=%async_computation.2 | async-start | bytes 7340032 | tf_op jit(solution)/shard_map/all_to_all | solution.py:105
  228.6 53.7 %all-to-all-start.1 = ((bf16[8,112,2048]{2,1,0:T(8,128)(2,1)}), bf16[8,112,2048]{2,1,0:T(8,128)(2,1)}, u32[]{:S(2)}, u32[]{:S(2)}) async-start(bf16[8,112,2048]{2,1,0:T(8,128)(2,1)} %bitcast.51), calls=%async_computation.1 | async-start | bytes 7340032 | tf_op jit(solution)/shard_map/all_to_all | solution.py:105
  282.3 3.0 copy-start.1
  282.3 3.0 copy-start.2
  282.3 3.4 %copy-start.3 = (f32[1,112,6144]{2,1,0:T(8,128)S(1)}, f32[1,112,6144]{2,1,0:T(8,128)}, u32[]{:S(2)}) copy-start(f32[1,112,6144]{2,1,0:T(8,128)} %param.8) | copy-start | bytes 8257540
  286.6 15.0 %collective-permute-start = (f32[112,2048]{1,0:T(8,128)S(1)}, f32[112,2048]{1,0:T(8,128)S(1)}, u32[]{:S(2)}, u32[]{:S(2)}) collective-permute-start(f32[112,2048]{1,0:T(8,128)S(1)} %get-tuple-element.5), channel_id=1, source_target_pairs={{0,8},{8,16},{16,24},{24,32},{32,40},{40,48},{48,56},{56,64},{64,7... | collective-permute-start | bytes 2752520 | tf_op jit(solution)/shard_map/ppermute | solution.py:19
  286.7 24.7 %collective-permute-start.1 = (f32[112,2048]{1,0:T(8,128)S(1)}, f32[112,2048]{1,0:T(8,128)S(1)}, u32[]{:S(2)}, u32[]{:S(2)}) collective-permute-start(f32[112,2048]{1,0:T(8,128)S(1)} %get-tuple-element.7), channel_id=1, source_target_pairs={{0,8},{8,16},{16,24},{24,32},{32,40},{40,48},{48,56},{56,64},{64,7... | collective-permute-start | bytes 2752520 | tf_op jit(solution)/shard_map/ppermute | solution.py:19
  287.7 33.6 %collective-permute-start.2 = (f32[112,2048]{1,0:T(8,128)S(1)}, f32[112,2048]{1,0:T(8,128)S(1)}, u32[]{:S(2)}, u32[]{:S(2)}) collective-permute-start(f32[112,2048]{1,0:T(8,128)S(1)} %get-tuple-element.6), channel_id=1, source_target_pairs={{0,8},{8,16},{16,24},{24,32},{32,40},{40,48},{48,56},{56,64},{64,7... | collective-permute-start | bytes 2752520 | tf_op jit(solution)/shard_map/ppermute | solution.py:19

commit v4 on v3

--- a/solution.py
+++ b/solution.py
@@ -88,12 +88,15 @@
     grouped = qkv[0].reshape(own_rows, 3, devices, local_width).transpose(2, 0, 1, 3)
     spread = lax.all_to_all(grouped, "sp", 0, 0, tiled=True)
     spread = spread.reshape(devices, own_rows, 3 * local_width)
+    resid_prev = passed_along(resid[0], "section", 1)
+    gate_prev = passed_along(gate[0], "section", 1)
+    resid_prev, gate_prev, spread = lax.optimization_barrier((resid_prev, gate_prev, spread))
     heads_all = attend_all(key_bias, spread, cache_kv[0], local_heads)
 
     device_place = lax.axis_index("sp")
     video_of = (device_place * own_rows + jnp.arange(own_rows, dtype=jnp.int32)) // SPAN
     picker = (video_of[:, None] == jnp.arange(VIDS, dtype=jnp.int32)[None, :]).astype(jnp.float32)
-    gains = jnp.dot(picker, gate[0], precision=lax.Precision.HIGHEST)
+    gains = jnp.dot(picker, gate_prev, precision=lax.Precision.HIGHEST)
     width = out_proj.shape[2]
     pieces = 3
     step = width // pieces
@@ -104,8 +107,9 @@
         shares = partial.astype(jnp.bfloat16).reshape(devices, own_rows, step)
         shares = lax.all_to_all(shares, "sp", 0, 0, tiled=True)
         projected = jnp.sum(shares.astype(jnp.float32), axis=0)
-        layer_out = resid[0, :, cols] + gains[:, cols] * projected
-        outs.append(passed_along(layer_out, "section", 1))
+        projected = lax.reduce_precision(projected, 8, 7).astype(jnp.bfloat16)
+        projected_prev = passed_along(projected, "section", 1).astype(jnp.float32)
+        outs.append(resid_prev[:, cols] + gains[:, cols] * projected_prev)
     return jnp.concatenate(outs, axis=1)[None]
 
 

time: 324 us -> 335 us (1.034); the launches traced: 323 us -> 329 us
  starting transfers between devices: 30.1 us -> 42.5 us
  waiting for transfers between devices: 206 us -> 198 us
    ppermute x3 -> x5, starting transfers between devices: 1.16 us -> 12.3 us  [passed_along(): lax.ppermute(shard, axis, [(i, (i + by) % devices) for i in range(devices)])]
    ppermute x3 -> x5, waiting for transfers between devices: 33.5 us -> 25.5 us  [passed_along(): lax.ppermute(shard, axis, [(i, (i + by) % devices) for i in range(devices)])]
    optimization_barrier x0 -> x1, local copies, waits for them, and re-layouts: none -> 6.6 us  [per_device(): lax.optimization_barrier((resid_prev, gate_prev, spread))]
    reshape x1 -> x0, local copies, waits for them, and re-layouts: 6.6 us -> none  [per_device(): spread = spread.reshape(devices, own_rows, 3 * local_width)]
  transfers between devices with their start and end apart: 7 -> 9, of which waited for: 7 -> 5; matrix products, arithmetic and copies ran while one was open for 7% -> 10% of each run, Pallas kernels for 0% -> 0%
where the time goes in v4:
time: 335 us; the launch traced here: 329 us
  waiting for transfers between devices  198 us (59%)
  starting transfers between devices  42.5 us (13%)
  Pallas kernels  30 us (9%)
  matrix products  22.8 us (7%)
  local copies, waits for them, and re-layouts  20 us (6%)
  other arithmetic  14.7 us (4%)
    all_to_all x3, waiting for transfers between devices, per_device(): shares = lax.all_to_all(shares, 'sp', 0, 0, tiled=True)  116 us
    all_to_all x1, waiting for transfers between devices, per_device(): spread = lax.all_to_all(grouped, 'sp', 0, 0, tiled=True)  56.9 us
    pallas_call x1, Pallas kernels, attend_all(): pl.pallas_call(attend_kernel, grid=(VIDS, local_heads), in_specs=[pl.Bloc...  30 us
    ppermute x5, waiting for transfers between devices, passed_along(): lax.ppermute(shard, axis, [(i, (i + by) % devices) for i in range(devices)])  25.5 us
    all_to_all x3, starting transfers between devices, per_device(): shares = lax.all_to_all(shares, 'sp', 0, 0, tiled=True)  22 us
    dot_general x3, matrix products, per_device(): jnp.dot(heads_all, out_proj[0, :, cols], preferred_element_type=jnp.float32)  21.6 us
    ppermute x5, starting transfers between devices, passed_along(): lax.ppermute(shard, axis, [(i, (i + by) % devices) for i in range(devices)])  12.3 us
    reduce_sum x3, other arithmetic, per_device(): projected = jnp.sum(shares.astype(jnp.float32), axis=0)  8.42 us
  transfers between devices with their start and end apart: 9, of which 5 were waited for; matrix products, arithmetic and copies ran while one was open for 10% of the time, Pallas kernels for 0%

profile of v4, /device:TPU:6, one launch (start us, length us, event | category | flops | bytes accessed | tf_op | source)
XLA Modules:
  0.0 329.5 jit_solution(11371573348123012826)
XLA Ops:
  0.0 0.0 copy-start
  0.0 3.4 %copy.28 = bf16[42,8,8,768]{3,2,1,0:T(8,128)(2,1)S(1)} copy(bf16[42,8,8,768]{3,1,2,0:T(8,128)(2,1)} %bitcast.44) | data formatting | bytes 8257536
  3.4 2.7 copy.23
  6.1 0.0 copy-start.2
  6.1 8.2 %all-to-all-start = ((bf16[8,112,3,768]{3,1,2,0:T(8,128)(2,1)}), bf16[8,112,3,768]{3,1,2,0:T(8,128)(2,1)}, u32[]{:S(2)}, u32[]{:S(2)}) async-start(bf16[8,112,3,768]{3,1,2,0:T(8,128)(2,1)} %copy.23), calls=%async_computation | async-start | bytes 8257536 | tf_op jit(solution)/shard_map/all_to_all | solution.py:89
  14.3 0.0 collective-permute-start
  14.3 0.0 copy-done.2
  14.3 1.1 collective-permute-start.1
  16.8 0.0 copy-done
  16.8 0.2 select_reduce_fusion
  17.0 0.1 broadcast_in_dim.38
  17.1 0.7 broadcast_in_dim_reshape.3.bias_ref
  17.8 56.9 %all-to-all-done = bf16[8,112,3,768]{3,1,2,0:T(8,128)(2,1)} async-done(((bf16[8,112,3,768]{3,1,2,0:T(8,128)(2,1)}), bf16[8,112,3,768]{3,1,2,0:T(8,128)(2,1)}, u32[]{:S(2)}, u32[]{:S(2)}) %all-to-all-start) | async-done | bytes 4128800 | tf_op jit(solution)/shard_map/all_to_all | solution.py:89
  74.7 6.5 %copy.24 = bf16[8,112,3,768]{1,3,2,0:T(8,128)(2,1)} copy(bf16[8,112,3,768]{3,1,2,0:T(8,128)(2,1)} %all-to-all-done) | data formatting | bytes 8257536 | tf_op jit(solution)/shard_map/all_to_all | solution.py:89
  81.2 0.0 collective-permute-done.1
  81.2 0.0 collective-permute-done
  81.2 6.6 %copy.25.q_ref.kn_ref.vn_ref = bf16[8,112,2304]{2,1,0:T(8,128)(2,1)} copy(bf16[8,112,2304]{1,2,0:T(8,128)(2,1)} %bitcast.42) | data formatting | bytes 8257536 | tf_op jit(solution)/shard_map/optimization_barrier | solution.py:93
  87.8 30.0 %shard_map.82 = bf16[896,768]{1,0:T(8,128)(2,1)} custom-call(f32[1,1344]{1,0:T(1,128)} %broadcast_in_dim_reshape.3.bias_ref, bf16[8,112,2304]{2,1,0:T(8,128)(2,1)} %copy.25.q_ref.kn_ref.vn_ref, bf16[8,112,2304]{2,1,0:T(8,128)(2,1)} %copy.25.q_ref.kn_ref.vn_ref, bf16[8,112,2304]{2,1,0:T(8,128)(2,1)} %copy.25.q_ref.kn_ref.vn_ref, ...), custom_call_target="tpu_custom_call" | custom-call | tf_op jit(solution)/shard_map/pallas_call | solution.py:63
  117.8 7.2 %convolution_convert_fusion.2 = bf16[896,2048]{1,0:T(8,128)(2,1)} fusion(bf16[896,768]{1,0:T(8,128)(2,1)} %shard_map.82, bf16[1,768,6144]{2,1,0:T(8,128)(2,1)} %param.11), kind=kOutput, calls=%fused_computation.5 | convolution fusion | flops 2820407296 | bytes 8192000 | tf_op jit(solution)/shard_map/dot_general | solution.py:106
  124.9 6.9 %all-to-all-start.1 = ((bf16[8,112,2048]{2,1,0:T(8,128)(2,1)}), bf16[8,112,2048]{2,1,0:T(8,128)(2,1)}, u32[]{:S(2)}, u32[]{:S(2)}) async-start(bf16[8,112,2048]{2,1,0:T(8,128)(2,1)} %bitcast.47), calls=%async_computation.1 | async-start | bytes 7340032 | tf_op jit(solution)/shard_map/all_to_all | solution.py:108
  131.8 7.2 %convolution_convert_fusion.1 = bf16[896,2048]{1,0:T(8,128)(2,1)} fusion(bf16[896,768]{1,0:T(8,128)(2,1)} %shard_map.82, bf16[1,768,6144]{2,1,0:T(8,128)(2,1)} %param.11), kind=kOutput, calls=%fused_computation.4 | convolution fusion | flops 2820407296 | bytes 8192000 | tf_op jit(solution)/shard_map/dot_general | solution.py:106
  139.1 35.4 %all-to-all-done.1 = bf16[8,112,2048]{2,1,0:T(8,128)(2,1)} async-done(((bf16[8,112,2048]{2,1,0:T(8,128)(2,1)}), bf16[8,112,2048]{2,1,0:T(8,128)(2,1)}, u32[]{:S(2)}, u32[]{:S(2)}) %all-to-all-start.1) | async-done | bytes 3670048 | tf_op jit(solution)/shard_map/all_to_all | solution.py:108
  174.5 8.2 %all-to-all-start.2 = ((bf16[8,112,2048]{2,1,0:T(8,128)(2,1)}), bf16[8,112,2048]{2,1,0:T(8,128)(2,1)}, u32[]{:S(2)}, u32[]{:S(2)}) async-start(bf16[8,112,2048]{2,1,0:T(8,128)(2,1)} %bitcast.46), calls=%async_computation.2 | async-start | bytes 7340032 | tf_op jit(solution)/shard_map/all_to_all | solution.py:108
  182.6 7.2 %convolution_convert_fusion = bf16[896,2048]{1,0:T(8,128)(2,1)} fusion(bf16[896,768]{1,0:T(8,128)(2,1)} %shard_map.82, bf16[1,768,6144]{2,1,0:T(8,128)(2,1)} %param.11), kind=kOutput, calls=%fused_computation.3 | convolution fusion | flops 2820407296 | bytes 8192000 | tf_op jit(solution)/shard_map/dot_general | solution.py:106
  189.8 47.6 %all-to-all-done.2 = bf16[8,112,2048]{2,1,0:T(8,128)(2,1)} async-done(((bf16[8,112,2048]{2,1,0:T(8,128)(2,1)}), bf16[8,112,2048]{2,1,0:T(8,128)(2,1)}, u32[]{:S(2)}, u32[]{:S(2)}) %all-to-all-start.2) | async-done | bytes 3670048 | tf_op jit(solution)/shard_map/all_to_all | solution.py:108
  237.4 6.9 %all-to-all-start.3 = ((bf16[8,112,2048]{2,1,0:T(8,128)(2,1)}), bf16[8,112,2048]{2,1,0:T(8,128)(2,1)}, u32[]{:S(2)}, u32[]{:S(2)}) async-start(bf16[8,112,2048]{2,1,0:T(8,128)(2,1)} %bitcast.45), calls=%async_computation.3 | async-start | bytes 7340032 | tf_op jit(solution)/shard_map/all_to_all | solution.py:108
  244.3 2.8 convert_reduce_fusion.2
  247.1 0.8 reduce-precision_convert_fusion.2
  248.0 0.0 collective-permute-start.2
  248.0 2.8 convert_reduce_fusion.1
  250.8 0.8 reduce-precision_convert_fusion.1
  251.6 11.1 %collective-permute-start.3 = (bf16[112,2048]{1,0:T(8,128)(2,1)}, bf16[112,2048]{1,0:T(8,128)(2,1)}, u32[]{:S(2)}, u32[]{:S(2)}) collective-permute-start(bf16[112,2048]{1,0:T(8,128)(2,1)} %reduce-precision_convert_fusion.1), channel_id=1, source_target_pairs={{0,8},{8,16},{16,24},{24,32},{32,40},{40,48},{48,56},{56,64},{64,7... | collective-permute-start | bytes 1376264 | tf_op jit(solution)/shard_map/ppermute | solution.py:19
  262.7 32.7 %all-to-all-done.3 = bf16[8,112,2048]{2,1,0:T(8,128)(2,1)} async-done(((bf16[8,112,2048]{2,1,0:T(8,128)(2,1)}), bf16[8,112,2048]{2,1,0:T(8,128)(2,1)}, u32[]{:S(2)}, u32[]{:S(2)}) %all-to-all-start.3) | async-done | bytes 3670048 | tf_op jit(solution)/shard_map/all_to_all | solution.py:108
  295.4 2.8 convert_reduce_fusion
  298.2 0.8 reduce-precision_convert_fusion
  299.1 0.0 collective-permute-start.4
  299.1 1.3 fusion.9
  300.4 0.0 collective-permute-done.2
  300.4 0.0 collective-permute-done.3
  300.4 25.5 %collective-permute-done.4 = bf16[112,2048]{1,0:T(8,128)(2,1)} collective-permute-done((bf16[112,2048]{1,0:T(8,128)(2,1)}, bf16[112,2048]{1,0:T(8,128)(2,1)}, u32[]{:S(2)}, u32[]{:S(2)}) %collective-permute-start.4) | collective-permute-done | bytes 458784 | tf_op jit(solution)/shard_map/ppermute | solution.py:19
  325.9 0.0 copy-start.1
  325.9 1.9 fusion.8
  327.7 1.7 maximum_bitcast_fusion
  329.5 0.0 copy-done.1
  (4 shorter events, 0.0 us)
Async XLA Ops:
  0.0 16.8 %copy-start = (s32[40,40]{1,0:T(8,128)S(1)}, s32[40,40]{1,0:T(8,128)}, u32[]{:S(2)}) copy-start(s32[40,40]{1,0:T(8,128)} %param.15) | copy-start | bytes 19204
  6.1 8.2 %copy-start.2 = (f32[1,2,6144]{2,1,0:T(2,128)S(1)}, f32[1,2,6144]{2,1,0:T(2,128)}, u32[]{:S(2)}) copy-start(f32[1,2,6144]{2,1,0:T(2,128)} %param.12) | copy-start | bytes 147460
  6.1 68.6 %all-to-all-start = ((bf16[8,112,3,768]{3,1,2,0:T(8,128)(2,1)}), bf16[8,112,3,768]{3,1,2,0:T(8,128)(2,1)}, u32[]{:S(2)}, u32[]{:S(2)}) async-start(bf16[8,112,3,768]{3,1,2,0:T(8,128)(2,1)} %copy.23), calls=%async_computation | async-start | bytes 8257536 | tf_op jit(solution)/shard_map/all_to_all | solution.py:89
  14.3 66.9 %collective-permute-start = (f32[112,6144]{1,0:T(8,128)}, f32[112,6144]{1,0:T(8,128)S(1)}, u32[]{:S(2)}, u32[]{:S(2)}) collective-permute-start(f32[112,6144]{1,0:T(8,128)} %bitcast.48), channel_id=1, source_target_pairs={{0,8},{8,16},{16,24},{24,32},{32,40},{40,48},{48,56},{56,64},{64,7... | collective-permute-start | bytes 8257544 | tf_op jit(solution)/shard_map/ppermute | solution.py:19
  14.3 66.9 %collective-permute-start.1 = (f32[2,6144]{1,0:T(2,128)S(1)}, f32[2,6144]{1,0:T(2,128)S(1)}, u32[]{:S(2)}, u32[]{:S(2)}) collective-permute-start(f32[2,6144]{1,0:T(2,128)S(1)} %bitcast.49), channel_id=1, source_target_pairs={{0,8},{8,16},{16,24},{24,32},{32,40},{40,48},{48,56},{56,64},{64,7... | collective-permute-start | bytes 147464 | tf_op jit(solution)/shard_map/ppermute | solution.py:19
  124.9 49.5 %all-to-all-start.1 = ((bf16[8,112,2048]{2,1,0:T(8,128)(2,1)}), bf16[8,112,2048]{2,1,0:T(8,128)(2,1)}, u32[]{:S(2)}, u32[]{:S(2)}) async-start(bf16[8,112,2048]{2,1,0:T(8,128)(2,1)} %bitcast.47), calls=%async_computation.1 | async-start | bytes 7340032 | tf_op jit(solution)/shard_map/all_to_all | solution.py:108
  174.5 62.9 %all-to-all-start.2 = ((bf16[8,112,2048]{2,1,0:T(8,128)(2,1)}), bf16[8,112,2048]{2,1,0:T(8,128)(2,1)}, u32[]{:S(2)}, u32[]{:S(2)}) async-start(bf16[8,112,2048]{2,1,0:T(8,128)(2,1)} %bitcast.46), calls=%async_computation.2 | async-start | bytes 7340032 | tf_op jit(solution)/shard_map/all_to_all | solution.py:108
  237.4 58.0 %all-to-all-start.3 = ((bf16[8,112,2048]{2,1,0:T(8,128)(2,1)}), bf16[8,112,2048]{2,1,0:T(8,128)(2,1)}, u32[]{:S(2)}, u32[]{:S(2)}) async-start(bf16[8,112,2048]{2,1,0:T(8,128)(2,1)} %bitcast.45), calls=%async_computation.3 | async-start | bytes 7340032 | tf_op jit(solution)/shard_map/all_to_all | solution.py:108
  248.0 52.4 %collective-permute-start.2 = (bf16[112,2048]{1,0:T(8,128)(2,1)}, bf16[112,2048]{1,0:T(8,128)(2,1)S(1)}, u32[]{:S(2)}, u32[]{:S(2)}) collective-permute-start(bf16[112,2048]{1,0:T(8,128)(2,1)} %reduce-precision_convert_fusion.2), channel_id=1, source_target_pairs={{0,8},{8,16},{16,24},{24,32},{32,40},{40,48},{48,56},{56,64},{64,7... | collective-permute-start | bytes 1376264 | tf_op jit(solution)/shard_map/ppermute | solution.py:19
  251.6 48.8 %collective-permute-start.3 = (bf16[112,2048]{1,0:T(8,128)(2,1)}, bf16[112,2048]{1,0:T(8,128)(2,1)}, u32[]{:S(2)}, u32[]{:S(2)}) collective-permute-start(bf16[112,2048]{1,0:T(8,128)(2,1)} %reduce-precision_convert_fusion.1), channel_id=1, source_target_pairs={{0,8},{8,16},{16,24},{24,32},{32,40},{40,48},{48,56},{56,64},{64,7... | collective-permute-start | bytes 1376264 | tf_op jit(solution)/shard_map/ppermute | solution.py:19
  299.1 26.8 %collective-permute-start.4 = (bf16[112,2048]{1,0:T(8,128)(2,1)}, bf16[112,2048]{1,0:T(8,128)(2,1)}, u32[]{:S(2)}, u32[]{:S(2)}) collective-permute-start(bf16[112,2048]{1,0:T(8,128)(2,1)} %reduce-precision_convert_fusion), channel_id=1, source_target_pairs={{0,8},{8,16},{16,24},{24,32},{32,40},{40,48},{48,56},{56,64},{64,7... | collective-permute-start | bytes 1376264 | tf_op jit(solution)/shard_map/ppermute | solution.py:19
  325.9 3.6 %copy-start.1 = (s32[40,40]{1,0:T(8,128)S(1)}, s32[40,40]{1,0:T(8,128)}, u32[]{:S(2)}) copy-start(s32[40,40]{1,0:T(8,128)} %param.15) | copy-start | bytes 19204

commit v5 on v3

--- a/solution.py
+++ b/solution.py
@@ -28,27 +28,32 @@
     return (slot_ids < filled) & (looked == 1)
 
 
-def attend_kernel(bias_ref, q_ref, kn_ref, vn_ref, kc_ref, vc_ref, out_ref):
+def attend_kernel(bias_ref, own_ref, kc_ref, vc_ref, out_ref):
     score_scale = HDIM ** (-0.5)
-    q = q_ref[...].reshape(SPAN, HDIM)
-    kn = kn_ref[...].reshape(SPAN, HDIM)
-    vn = vn_ref[...].reshape(SPAN, HDIM)
-    kc = kc_ref[0, 0]
-    vc = vc_ref[0, 0]
+    local_heads = out_ref.shape[1] // HDIM
+    width = local_heads * HDIM
     contract = (((1,), (1,)), ((), ()))
-    far = lax.dot_general(q, kc, contract, preferred_element_type=jnp.float32) * score_scale
-    far = far + bias_ref[...]
-    near = lax.dot_general(q, kn, contract, preferred_element_type=jnp.float32) * score_scale
-    highest = jnp.maximum(jnp.max(far, axis=1, keepdims=True), jnp.max(near, axis=1, keepdims=True))
-    far_raised = jnp.exp(far - highest)
-    near_raised = jnp.exp(near - highest)
-    total = jnp.sum(far_raised, axis=1, keepdims=True) + jnp.sum(near_raised, axis=1, keepdims=True)
-    far_w = (far_raised / total).astype(jnp.bfloat16)
-    near_w = (near_raised / total).astype(jnp.bfloat16)
-    mixed = jnp.dot(far_w, vc, preferred_element_type=jnp.float32) + jnp.dot(
-        near_w, vn, preferred_element_type=jnp.float32
-    )
-    out_ref[...] = mixed.astype(out_ref.dtype)
+    bias = bias_ref[...]
+    for h in range(local_heads):
+        cols = slice(h * HDIM, (h + 1) * HDIM)
+        q = own_ref[:, :, h * HDIM:(h + 1) * HDIM].reshape(SPAN, HDIM)
+        kn = own_ref[:, :, width + h * HDIM:width + (h + 1) * HDIM].reshape(SPAN, HDIM)
+        vn = own_ref[:, :, 2 * width + h * HDIM:2 * width + (h + 1) * HDIM].reshape(SPAN, HDIM)
+        kc = kc_ref[0, 0, :, cols]
+        vc = vc_ref[0, 0, :, cols]
+        far = lax.dot_general(q, kc, contract, preferred_element_type=jnp.float32) * score_scale
+        far = far + bias
+        near = lax.dot_general(q, kn, contract, preferred_element_type=jnp.float32) * score_scale
+        highest = jnp.maximum(jnp.max(far, axis=1, keepdims=True), jnp.max(near, axis=1, keepdims=True))
+        far_raised = jnp.exp(far - highest)
+        near_raised = jnp.exp(near - highest)
+        total = jnp.sum(far_raised, axis=1, keepdims=True) + jnp.sum(near_raised, axis=1, keepdims=True)
+        far_w = (far_raised / total).astype(jnp.bfloat16)
+        near_w = (near_raised / total).astype(jnp.bfloat16)
+        mixed = jnp.dot(far_w, vc, preferred_element_type=jnp.float32) + jnp.dot(
+            near_w, vn, preferred_element_type=jnp.float32
+        )
+        out_ref[:, cols] = mixed.astype(out_ref.dtype)
 
 
 def attend_all(key_bias, spread, cache_kv, local_heads):
@@ -57,23 +62,18 @@
     rows = spread.shape[1]
     width = local_heads * HDIM
 
-    def own_spec(part):
-        return pl.BlockSpec((per_video, rows, HDIM), lambda b, h: (b, 0, part * local_heads + h))
-
     return pl.pallas_call(
         attend_kernel,
-        grid=(VIDS, local_heads),
+        grid=(VIDS,),
         in_specs=[
-            pl.BlockSpec((1, KEYS), lambda b, h: (0, 0)),
-            own_spec(0),
-            own_spec(1),
-            own_spec(2),
-            pl.BlockSpec((1, 1, KEYS, HDIM), lambda b, h: (0, b, 0, h)),
-            pl.BlockSpec((1, 1, KEYS, HDIM), lambda b, h: (1, b, 0, h)),
+            pl.BlockSpec((1, KEYS), lambda b: (0, 0)),
+            pl.BlockSpec((per_video, rows, 3 * width), lambda b: (b, 0, 0)),
+            pl.BlockSpec((1, 1, KEYS, width), lambda b: (0, b, 0, 0)),
+            pl.BlockSpec((1, 1, KEYS, width), lambda b: (1, b, 0, 0)),
         ],
-        out_specs=pl.BlockSpec((SPAN, HDIM), lambda b, h: (b, h)),
+        out_specs=pl.BlockSpec((SPAN, width), lambda b: (b, 0)),
         out_shape=jax.ShapeDtypeStruct((TOKS, width), jnp.bfloat16),
-    )(key_bias, spread, spread, spread, cache_kv, cache_kv)
+    )(key_bias, spread, cache_kv, cache_kv)
 
 
 def per_device(resid, qkv, cache_kv, out_proj, gate, span_ids, cache_counts, span_mask):
@@ -86,8 +86,8 @@
     key_bias = jnp.repeat(jnp.where(live_slots, 0.0, -jnp.inf).astype(jnp.float32), SPAN)[None, :]
 
     grouped = qkv[0].reshape(own_rows, 3, devices, local_width).transpose(2, 0, 1, 3)
+    grouped = grouped.reshape(devices, own_rows, 3 * local_width)
     spread = lax.all_to_all(grouped, "sp", 0, 0, tiled=True)
-    spread = spread.reshape(devices, own_rows, 3 * local_width)
     heads_all = attend_all(key_bias, spread, cache_kv[0], local_heads)
 
     device_place = lax.axis_index("sp")

time: 324 us -> 320 us (0.988)
  Pallas kernels: 30 us -> 26.3 us
    another operation x0 -> x1, local copies, waits for them, and re-layouts: none -> 6.75 us  [per_device(): qkv[0].reshape(own_rows, 3, devices, local_width).transpose(2, 0, 1, 3)]
    all_to_all x1 -> x0, local copies, waits for them, and re-layouts: 6.49 us -> none  [per_device(): spread = lax.all_to_all(grouped, 'sp', 0, 0, tiled=True)]
    pallas_call x1, Pallas kernels: 30 us -> 26.3 us  [attend_all(): pl.pallas_call(attend_kernel, grid=(VIDS,), in_specs=[pl.BlockSpec((1, KE...]
where the time goes in v5:
time: 320 us; the launch traced here: 319 us
  waiting for transfers between devices  206 us (64%)
  starting transfers between devices  30.1 us (9%)
  Pallas kernels  26.3 us (8%)
  matrix products  21.1 us (7%)
  local copies, waits for them, and re-layouts  20.7 us (6%)
  other arithmetic  13.1 us (4%)
    all_to_all x3, waiting for transfers between devices, per_device(): shares = lax.all_to_all(shares, 'sp', 0, 0, tiled=True)  115 us
    all_to_all x1, waiting for transfers between devices, per_device(): spread = lax.all_to_all(grouped, 'sp', 0, 0, tiled=True)  57.3 us
    ppermute x3, waiting for transfers between devices, passed_along(): lax.ppermute(shard, axis, [(i, (i + by) % devices) for i in range(devices)])  33.5 us
    pallas_call x1, Pallas kernels, attend_all(): pl.pallas_call(attend_kernel, grid=(VIDS,), in_specs=[pl.BlockSpec((1, KE...  26.3 us
    all_to_all x3, starting transfers between devices, per_device(): shares = lax.all_to_all(shares, 'sp', 0, 0, tiled=True)  20.9 us
    dot_general x3, matrix products, per_device(): jnp.dot(heads_all, out_proj[0, :, cols], preferred_element_type=jnp.float32)  19.8 us
    reduce_sum x3, other arithmetic, per_device(): projected = jnp.sum(shares.astype(jnp.float32), axis=0)  10.4 us
    all_to_all x1, starting transfers between devices, per_device(): spread = lax.all_to_all(grouped, 'sp', 0, 0, tiled=True)  8.09 us
  transfers between devices with their start and end apart: 7, of which 7 were waited for; matrix products, arithmetic and copies ran while one was open for 7% of the time, Pallas kernels for 0%

profile of v5, /device:TPU:6, one launch (start us, length us, event | category | flops | bytes accessed | tf_op | source)
XLA Modules:
  0.0 318.9 jit_solution(14387522826098219809)
XLA Ops:
  0.0 0.0 copy-start
  0.0 5.4 %copy.14 = bf16[42,8,8,768]{3,2,1,0:T(8,128)(2,1)} copy(bf16[42,8,8,768]{3,1,2,0:T(8,128)(2,1)} %bitcast.50) | data formatting | bytes 8257536
  5.4 6.7 %copy.12 = bf16[112,3,8,768]{0,3,1,2:T(8,128)(2,1)} copy(bf16[112,3,8,768]{3,2,0,1:T(8,128)(2,1)} %bitcast.49) | data formatting | bytes 8257536 | tf_op jit(solution)/shard_map/reshape;squeeze | solution.py:88
  12.2 6.6 %copy.13 = bf16[8,112,2304]{2,1,0:T(8,128)(2,1)} copy(bf16[8,112,2304]{1,2,0:T(8,128)(2,1)} %bitcast.48) | data formatting | bytes 8257536 | tf_op jit(solution)/shard_map/reshape | solution.py:89
  18.7 8.1 %all-to-all-start = ((bf16[8,112,2304]{2,1,0:T(8,128)(2,1)}), bf16[8,112,2304]{2,1,0:T(8,128)(2,1)}, u32[]{:S(2)}, u32[]{:S(2)}) async-start(bf16[8,112,2304]{2,1,0:T(8,128)(2,1)} %copy.13), calls=%async_computation | async-start | bytes 8257536 | tf_op jit(solution)/shard_map/all_to_all | solution.py:90
  28.2 0.7 dynamic-slice_bitcast_fusion
  28.9 0.2 select_reduce_fusion
  29.0 0.1 broadcast_in_dim.38
  29.1 0.7 broadcast_in_dim_reshape.3.bias_ref
  29.8 57.3 %all-to-all-done.own_ref = bf16[8,112,2304]{2,1,0:T(8,128)(2,1)} async-done(((bf16[8,112,2304]{2,1,0:T(8,128)(2,1)}), bf16[8,112,2304]{2,1,0:T(8,128)(2,1)}, u32[]{:S(2)}, u32[]{:S(2)}) %all-to-all-start) | async-done | bytes 4128800 | tf_op jit(solution)/shard_map/all_to_all | solution.py:90
  87.1 26.3 %shard_map.82 = bf16[896,768]{1,0:T(8,128)(2,1)} custom-call(f32[1,1344]{1,0:T(1,128)} %broadcast_in_dim_reshape.3.bias_ref, bf16[8,112,2304]{2,1,0:T(8,128)(2,1)} %all-to-all-done.own_ref, bf16[2,2,1344,768]{3,2,1,0:T(8,128)(2,1)} %bitcast.46, bf16[2,2,1344,768]{3,2,1,0:T(8,128)(2,1)} %bitcast.47), custom_call_target="tpu_custom_call" | custom-call | tf_op jit(solution)/shard_map/pallas_call | solution.py:65
  113.4 7.2 %convolution_convert_fusion = bf16[896,2048]{1,0:T(8,128)(2,1)} fusion(bf16[896,768]{1,0:T(8,128)(2,1)} %shard_map.82, bf16[1,768,6144]{2,1,0:T(8,128)(2,1)} %param.11), kind=kOutput, calls=%fused_computation.3 | convolution fusion | flops 2820407296 | bytes 8192000 | tf_op jit(solution)/shard_map/dot_general | solution.py:103
  120.6 0.0 copy-start.4
  120.6 7.0 %all-to-all-start.3 = ((bf16[8,112,2048]{2,1,0:T(8,128)(2,1)}), bf16[8,112,2048]{2,1,0:T(8,128)(2,1)}, u32[]{:S(2)}, u32[]{:S(2)}) async-start(bf16[8,112,2048]{2,1,0:T(8,128)(2,1)} %bitcast.53), calls=%async_computation.3 | async-start | bytes 7340032 | tf_op jit(solution)/shard_map/all_to_all | solution.py:105
  127.6 0.0 copy-done.4
  127.6 6.3 %convolution_convert_fusion.1 = bf16[896,2048]{1,0:T(8,128)(2,1)} fusion(bf16[896,768]{1,0:T(8,128)(2,1)S(1)} %copy-done.4, bf16[1,768,6144]{2,1,0:T(8,128)(2,1)} %param.11), kind=kOutput, calls=%fused_computation.4 | convolution fusion | flops 2820407296 | bytes 8192000 | tf_op jit(solution)/shard_map/dot_general | solution.py:103
  134.0 41.6 %all-to-all-done.3 = bf16[8,112,2048]{2,1,0:T(8,128)(2,1)} async-done(((bf16[8,112,2048]{2,1,0:T(8,128)(2,1)}), bf16[8,112,2048]{2,1,0:T(8,128)(2,1)}, u32[]{:S(2)}, u32[]{:S(2)}) %all-to-all-start.3) | async-done | bytes 3670048 | tf_op jit(solution)/shard_map/all_to_all | solution.py:105
  175.6 6.9 %all-to-all-start.2 = ((bf16[8,112,2048]{2,1,0:T(8,128)(2,1)}), bf16[8,112,2048]{2,1,0:T(8,128)(2,1)}, u32[]{:S(2)}, u32[]{:S(2)}) async-start(bf16[8,112,2048]{2,1,0:T(8,128)(2,1)} %bitcast.52), calls=%async_computation.2 | async-start | bytes 7340032 | tf_op jit(solution)/shard_map/all_to_all | solution.py:105
  182.5 6.3 %convolution_convert_fusion.2 = bf16[896,2048]{1,0:T(8,128)(2,1)} fusion(bf16[896,768]{1,0:T(8,128)(2,1)S(1)} %copy-done.4, bf16[1,768,6144]{2,1,0:T(8,128)(2,1)} %param.11), kind=kOutput, calls=%fused_computation.5 | convolution fusion | flops 2820407296 | bytes 8192000 | tf_op jit(solution)/shard_map/dot_general | solution.py:103
  188.8 35.7 %all-to-all-done.2 = bf16[8,112,2048]{2,1,0:T(8,128)(2,1)} async-done(((bf16[8,112,2048]{2,1,0:T(8,128)(2,1)}), bf16[8,112,2048]{2,1,0:T(8,128)(2,1)}, u32[]{:S(2)}, u32[]{:S(2)}) %all-to-all-start.2) | async-done | bytes 3670048 | tf_op jit(solution)/shard_map/all_to_all | solution.py:105
  224.5 6.9 %all-to-all-start.1 = ((bf16[8,112,2048]{2,1,0:T(8,128)(2,1)}), bf16[8,112,2048]{2,1,0:T(8,128)(2,1)}, u32[]{:S(2)}, u32[]{:S(2)}) async-start(bf16[8,112,2048]{2,1,0:T(8,128)(2,1)} %bitcast.51), calls=%async_computation.1 | async-start | bytes 7340032 | tf_op jit(solution)/shard_map/all_to_all | solution.py:105
  231.5 0.0 copy-done
  231.5 1.3 fusion.9
  232.8 3.7 %convert_reduce_fusion = f32[112,2048]{1,0:T(8,128)} fusion(bf16[8,112,2048]{2,1,0:T(8,128)(2,1)} %all-to-all-done.3), kind=kLoop, calls=%fused_computation | loop fusion | flops 3440640 | bytes 4587520 | tf_op jit(solution)/shard_map/reduce_sum | solution.py:106
  236.5 3.7 %convert_reduce_fusion.1 = f32[112,2048]{1,0:T(8,128)} fusion(bf16[8,112,2048]{2,1,0:T(8,128)(2,1)} %all-to-all-done.2), kind=kLoop, calls=%fused_computation.1 | loop fusion | flops 3440640 | bytes 4587520 | tf_op jit(solution)/shard_map/reduce_sum | solution.py:106
  240.2 38.1 %all-to-all-done.1 = bf16[8,112,2048]{2,1,0:T(8,128)(2,1)} async-done(((bf16[8,112,2048]{2,1,0:T(8,128)(2,1)}), bf16[8,112,2048]{2,1,0:T(8,128)(2,1)}, u32[]{:S(2)}, u32[]{:S(2)}) %all-to-all-start.1) | async-done | bytes 3670048 | tf_op jit(solution)/shard_map/all_to_all | solution.py:105
  278.3 0.0 copy-start.1
  278.3 0.0 copy-start.2
  278.3 0.0 copy-start.3
  278.3 3.0 convert_reduce_fusion.2
  281.2 0.0 copy-done.1
  281.2 0.0 copy-done.2
  281.3 0.4 copy-done.3
  281.7 0.8 fusion.8
  282.5 0.1 collective-permute-start
  282.6 1.0 collective-permute-start.1
  283.6 0.1 collective-permute-start.2
  283.7 13.8 %collective-permute-done = f32[112,2048]{1,0:T(8,128)S(1)} collective-permute-done((f32[112,2048]{1,0:T(8,128)S(1)}, f32[112,2048]{1,0:T(8,128)S(1)}, u32[]{:S(2)}, u32[]{:S(2)}) %collective-permute-start) | collective-permute-done | bytes 917536 | tf_op jit(solution)/shard_map/ppermute | solution.py:19
  297.5 9.8 %collective-permute-done.1 = f32[112,2048]{1,0:T(8,128)S(1)} collective-permute-done((f32[112,2048]{1,0:T(8,128)S(1)}, f32[112,2048]{1,0:T(8,128)S(1)}, u32[]{:S(2)}, u32[]{:S(2)}) %collective-permute-start.1) | collective-permute-done | bytes 917536 | tf_op jit(solution)/shard_map/ppermute | solution.py:19
  307.3 9.8 %collective-permute-done.2 = f32[112,2048]{1,0:T(8,128)S(1)} collective-permute-done((f32[112,2048]{1,0:T(8,128)S(1)}, f32[112,2048]{1,0:T(8,128)S(1)}, u32[]{:S(2)}, u32[]{:S(2)}) %collective-permute-start.2) | collective-permute-done | bytes 917536 | tf_op jit(solution)/shard_map/ppermute | solution.py:19
  317.2 1.7 maximum_bitcast_fusion
  (3 shorter events, 0.0 us)
Async XLA Ops:
  0.0 231.5 %copy-start = (f32[1,2,6144]{2,1,0:T(2,128)S(1)}, f32[1,2,6144]{2,1,0:T(2,128)}, u32[]{:S(2)}) copy-start(f32[1,2,6144]{2,1,0:T(2,128)} %param.12) | copy-start | bytes 147460
  18.7 68.3 %all-to-all-start = ((bf16[8,112,2304]{2,1,0:T(8,128)(2,1)}), bf16[8,112,2304]{2,1,0:T(8,128)(2,1)}, u32[]{:S(2)}, u32[]{:S(2)}) async-start(bf16[8,112,2304]{2,1,0:T(8,128)(2,1)} %copy.13), calls=%async_computation | async-start | bytes 8257536 | tf_op jit(solution)/shard_map/all_to_all | solution.py:90
  120.6 7.1 %copy-start.4 = (bf16[896,768]{1,0:T(8,128)(2,1)S(1)}, bf16[896,768]{1,0:T(8,128)(2,1)}, u32[]{:S(2)}) copy-start(bf16[896,768]{1,0:T(8,128)(2,1)} %shard_map.82) | copy-start | bytes 4128772
  120.6 55.0 %all-to-all-start.3 = ((bf16[8,112,2048]{2,1,0:T(8,128)(2,1)}), bf16[8,112,2048]{2,1,0:T(8,128)(2,1)}, u32[]{:S(2)}, u32[]{:S(2)}) async-start(bf16[8,112,2048]{2,1,0:T(8,128)(2,1)} %bitcast.53), calls=%async_computation.3 | async-start | bytes 7340032 | tf_op jit(solution)/shard_map/all_to_all | solution.py:105
  175.6 49.0 %all-to-all-start.2 = ((bf16[8,112,2048]{2,1,0:T(8,128)(2,1)}), bf16[8,112,2048]{2,1,0:T(8,128)(2,1)}, u32[]{:S(2)}, u32[]{:S(2)}) async-start(bf16[8,112,2048]{2,1,0:T(8,128)(2,1)} %bitcast.52), calls=%async_computation.2 | async-start | bytes 7340032 | tf_op jit(solution)/shard_map/all_to_all | solution.py:105
  224.5 53.7 %all-to-all-start.1 = ((bf16[8,112,2048]{2,1,0:T(8,128)(2,1)}), bf16[8,112,2048]{2,1,0:T(8,128)(2,1)}, u32[]{:S(2)}, u32[]{:S(2)}) async-start(bf16[8,112,2048]{2,1,0:T(8,128)(2,1)} %bitcast.51), calls=%async_computation.1 | async-start | bytes 7340032 | tf_op jit(solution)/shard_map/all_to_all | solution.py:105
  278.3 3.0 copy-start.1
  278.3 3.0 copy-start.2
  278.3 3.4 %copy-start.3 = (f32[1,112,6144]{2,1,0:T(8,128)S(1)}, f32[1,112,6144]{2,1,0:T(8,128)}, u32[]{:S(2)}) copy-start(f32[1,112,6144]{2,1,0:T(8,128)} %param.8) | copy-start | bytes 8257540
  282.5 15.0 %collective-permute-start = (f32[112,2048]{1,0:T(8,128)S(1)}, f32[112,2048]{1,0:T(8,128)S(1)}, u32[]{:S(2)}, u32[]{:S(2)}) collective-permute-start(f32[112,2048]{1,0:T(8,128)S(1)} %get-tuple-element.5), channel_id=1, source_target_pairs={{0,8},{8,16},{16,24},{24,32},{32,40},{40,48},{48,56},{56,64},{64,7... | collective-permute-start | bytes 2752520 | tf_op jit(solution)/shard_map/ppermute | solution.py:19
  282.6 24.7 %collective-permute-start.1 = (f32[112,2048]{1,0:T(8,128)S(1)}, f32[112,2048]{1,0:T(8,128)S(1)}, u32[]{:S(2)}, u32[]{:S(2)}) collective-permute-start(f32[112,2048]{1,0:T(8,128)S(1)} %get-tuple-element.7), channel_id=1, source_target_pairs={{0,8},{8,16},{16,24},{24,32},{32,40},{40,48},{48,56},{56,64},{64,7... | collective-permute-start | bytes 2752520 | tf_op jit(solution)/shard_map/ppermute | solution.py:19
  283.6 33.6 %collective-permute-start.2 = (f32[112,2048]{1,0:T(8,128)S(1)}, f32[112,2048]{1,0:T(8,128)S(1)}, u32[]{:S(2)}, u32[]{:S(2)}) collective-permute-start(f32[112,2048]{1,0:T(8,128)S(1)} %get-tuple-element.6), channel_id=1, source_target_pairs={{0,8},{8,16},{16,24},{24,32},{32,40},{40,48},{48,56},{56,64},{64,7... | collective-permute-start | bytes 2752520 | tf_op jit(solution)/shard_map/ppermute | solution.py:19

commit v6 on v5

--- a/solution.py
+++ b/solution.py
@@ -95,7 +95,7 @@
     picker = (video_of[:, None] == jnp.arange(VIDS, dtype=jnp.int32)[None, :]).astype(jnp.float32)
     gains = jnp.dot(picker, gate[0], precision=lax.Precision.HIGHEST)
     width = out_proj.shape[2]
-    pieces = 3
+    pieces = 4
     step = width // pieces
     outs = []
     for c in range(pieces):

time: 320 us -> 326 us (1.019)
  starting transfers between devices: 30.1 us -> 39.3 us
  waiting for transfers between devices: 206 us -> 198 us
  matrix products: 21.1 us -> 26.6 us
    all_to_all x3 -> x4, starting transfers between devices: 20.9 us -> 27.9 us  [per_device(): shares = lax.all_to_all(shares, 'sp', 0, 0, tiled=True)]
    all_to_all x3 -> x4, waiting for transfers between devices: 115 us -> 110 us  [per_device(): shares = lax.all_to_all(shares, 'sp', 0, 0, tiled=True)]
    dot_general x3 -> x4, matrix products: 19.8 us -> 23.7 us  [per_device(): jnp.dot(heads_all, out_proj[0, :, cols], preferred_element_type=jnp.float32)]
    ppermute x3 -> x4, waiting for transfers between devices: 33.5 us -> 31.3 us  [passed_along(): lax.ppermute(shard, axis, [(i, (i + by) % devices) for i in range(devices)])]
    reduce_sum x3 -> x4, other arithmetic: 10.4 us -> 9.04 us  [per_device(): projected = jnp.sum(shares.astype(jnp.float32), axis=0)]
  transfers between devices with their start and end apart: 7 -> 9, of which waited for: 7 -> 9; matrix products, arithmetic and copies ran while one was open for 7% -> 9% of each run, Pallas kernels for 0% -> 0%
where the time goes in v6:
time: 326 us
  waiting for transfers between devices  198 us (61%)
  starting transfers between devices  39.3 us (12%)
  matrix products  26.6 us (8%)
  Pallas kernels  26.4 us (8%)
  local copies, waits for them, and re-layouts  20.5 us (6%)
  other arithmetic  13 us (4%)
    all_to_all x4, waiting for transfers between devices, per_device(): shares = lax.all_to_all(shares, 'sp', 0, 0, tiled=True)  110 us
    all_to_all x1, waiting for transfers between devices, per_device(): spread = lax.all_to_all(grouped, 'sp', 0, 0, tiled=True)  57.3 us
    ppermute x4, waiting for transfers between devices, passed_along(): lax.ppermute(shard, axis, [(i, (i + by) % devices) for i in range(devices)])  31.3 us
    all_to_all x4, starting transfers between devices, per_device(): shares = lax.all_to_all(shares, 'sp', 0, 0, tiled=True)  27.9 us
    pallas_call x1, Pallas kernels, attend_all(): pl.pallas_call(attend_kernel, grid=(VIDS,), in_specs=[pl.BlockSpec((1, KE...  26.4 us
    dot_general x4, matrix products, per_device(): jnp.dot(heads_all, out_proj[0, :, cols], preferred_element_type=jnp.float32)  23.7 us
    reduce_sum x4, other arithmetic, per_device(): projected = jnp.sum(shares.astype(jnp.float32), axis=0)  9.04 us
    all_to_all x1, starting transfers between devices, per_device(): spread = lax.all_to_all(grouped, 'sp', 0, 0, tiled=True)  8.09 us
  transfers between devices with their start and end apart: 9, of which 9 were waited for; matrix products, arithmetic and copies ran while one was open for 9% of the time, Pallas kernels for 0%

profile of v6, /device:TPU:6, one launch (start us, length us, event | category | flops | bytes accessed | tf_op | source)
XLA Modules:
  0.0 325.6 jit_solution(640346459856121243)
XLA Ops:
  0.0 0.0 copy-start
  0.0 5.4 %copy.14 = bf16[42,8,8,768]{3,2,1,0:T(8,128)(2,1)} copy(bf16[42,8,8,768]{3,1,2,0:T(8,128)(2,1)} %bitcast.57) | data formatting | bytes 8257536
  5.4 6.8 %copy.12 = bf16[112,3,8,768]{0,3,1,2:T(8,128)(2,1)} copy(bf16[112,3,8,768]{3,2,0,1:T(8,128)(2,1)} %bitcast.56) | data formatting | bytes 8257536 | tf_op jit(solution)/shard_map/reshape;squeeze | solution.py:88
  12.2 6.5 %copy.13 = bf16[8,112,2304]{2,1,0:T(8,128)(2,1)} copy(bf16[8,112,2304]{1,2,0:T(8,128)(2,1)} %bitcast.55) | data formatting | bytes 8257536 | tf_op jit(solution)/shard_map/reshape | solution.py:89
  18.7 8.1 %all-to-all-start = ((bf16[8,112,2304]{2,1,0:T(8,128)(2,1)}), bf16[8,112,2304]{2,1,0:T(8,128)(2,1)}, u32[]{:S(2)}, u32[]{:S(2)}) async-start(bf16[8,112,2304]{2,1,0:T(8,128)(2,1)} %copy.13), calls=%async_computation | async-start | bytes 8257536 | tf_op jit(solution)/shard_map/all_to_all | solution.py:90
  28.1 0.7 dynamic-slice_bitcast_fusion
  28.8 0.2 select_reduce_fusion
  29.0 0.1 broadcast_in_dim.38
  29.1 0.7 broadcast_in_dim_reshape.3.bias_ref
  29.8 57.3 %all-to-all-done.own_ref = bf16[8,112,2304]{2,1,0:T(8,128)(2,1)} async-done(((bf16[8,112,2304]{2,1,0:T(8,128)(2,1)}), bf16[8,112,2304]{2,1,0:T(8,128)(2,1)}, u32[]{:S(2)}, u32[]{:S(2)}) %all-to-all-start) | async-done | bytes 4128800 | tf_op jit(solution)/shard_map/all_to_all | solution.py:90
  87.0 26.4 %shard_map.82 = bf16[896,768]{1,0:T(8,128)(2,1)} custom-call(f32[1,1344]{1,0:T(1,128)} %broadcast_in_dim_reshape.3.bias_ref, bf16[8,112,2304]{2,1,0:T(8,128)(2,1)} %all-to-all-done.own_ref, bf16[2,2,1344,768]{3,2,1,0:T(8,128)(2,1)} %bitcast.53, bf16[2,2,1344,768]{3,2,1,0:T(8,128)(2,1)} %bitcast.54), custom_call_target="tpu_custom_call" | custom-call | tf_op jit(solution)/shard_map/pallas_call | solution.py:65
  113.5 5.9 %convolution_convert_fusion = bf16[896,1536]{1,0:T(8,128)(2,1)} fusion(bf16[896,768]{1,0:T(8,128)(2,1)} %shard_map.82, bf16[1,768,6144]{2,1,0:T(8,128)(2,1)} %param.11), kind=kOutput, calls=%fused_computation.4 | convolution fusion | flops 2115305472 | bytes 6488064 | tf_op jit(solution)/shard_map/dot_general | solution.py:103
  119.4 6.9 %all-to-all-start.4 = ((bf16[8,112,1536]{2,1,0:T(8,128)(2,1)}), bf16[8,112,1536]{2,1,0:T(8,128)(2,1)S(1)}, u32[]{:S(2)}, u32[]{:S(2)}) async-start(bf16[8,112,1536]{2,1,0:T(8,128)(2,1)} %bitcast.61), calls=%async_computation.4 | async-start | bytes 5505024 | tf_op jit(solution)/shard_map/all_to_all | solution.py:105
  126.3 6.0 %convolution_convert_fusion.1 = bf16[896,1536]{1,0:T(8,128)(2,1)} fusion(bf16[896,768]{1,0:T(8,128)(2,1)} %shard_map.82, bf16[1,768,6144]{2,1,0:T(8,128)(2,1)} %param.11), kind=kOutput, calls=%fused_computation.5 | convolution fusion | flops 2115305472 | bytes 6488064 | tf_op jit(solution)/shard_map/dot_general | solution.py:103
  132.3 26.9 %all-to-all-done.4 = bf16[8,112,1536]{2,1,0:T(8,128)(2,1)S(1)} async-done(((bf16[8,112,1536]{2,1,0:T(8,128)(2,1)}), bf16[8,112,1536]{2,1,0:T(8,128)(2,1)S(1)}, u32[]{:S(2)}, u32[]{:S(2)}) %all-to-all-start.4) | async-done | bytes 2752544 | tf_op jit(solution)/shard_map/all_to_all | solution.py:105
  159.2 6.9 %all-to-all-start.3 = ((bf16[8,112,1536]{2,1,0:T(8,128)(2,1)}), bf16[8,112,1536]{2,1,0:T(8,128)(2,1)}, u32[]{:S(2)}, u32[]{:S(2)}) async-start(bf16[8,112,1536]{2,1,0:T(8,128)(2,1)} %bitcast.60), calls=%async_computation.3 | async-start | bytes 5505024 | tf_op jit(solution)/shard_map/all_to_all | solution.py:105
  166.1 5.9 %convolution_convert_fusion.2 = bf16[896,1536]{1,0:T(8,128)(2,1)} fusion(bf16[896,768]{1,0:T(8,128)(2,1)} %shard_map.82, bf16[1,768,6144]{2,1,0:T(8,128)(2,1)} %param.11), kind=kOutput, calls=%fused_computation.6 | convolution fusion | flops 2115305472 | bytes 6488064 | tf_op jit(solution)/shard_map/dot_general | solution.py:103
  172.0 27.8 %all-to-all-done.3 = bf16[8,112,1536]{2,1,0:T(8,128)(2,1)} async-done(((bf16[8,112,1536]{2,1,0:T(8,128)(2,1)}), bf16[8,112,1536]{2,1,0:T(8,128)(2,1)}, u32[]{:S(2)}, u32[]{:S(2)}) %all-to-all-start.3) | async-done | bytes 2752544 | tf_op jit(solution)/shard_map/all_to_all | solution.py:105
  199.8 7.0 %all-to-all-start.2 = ((bf16[8,112,1536]{2,1,0:T(8,128)(2,1)}), bf16[8,112,1536]{2,1,0:T(8,128)(2,1)}, u32[]{:S(2)}, u32[]{:S(2)}) async-start(bf16[8,112,1536]{2,1,0:T(8,128)(2,1)} %bitcast.59), calls=%async_computation.2 | async-start | bytes 5505024 | tf_op jit(solution)/shard_map/all_to_all | solution.py:105
  206.9 5.9 %convolution_convert_fusion.3 = bf16[896,1536]{1,0:T(8,128)(2,1)} fusion(bf16[896,768]{1,0:T(8,128)(2,1)} %shard_map.82, bf16[1,768,6144]{2,1,0:T(8,128)(2,1)} %param.11), kind=kOutput, calls=%fused_computation.7 | convolution fusion | flops 2115305472 | bytes 6488064 | tf_op jit(solution)/shard_map/dot_general | solution.py:103
  212.8 25.2 %all-to-all-done.2 = bf16[8,112,1536]{2,1,0:T(8,128)(2,1)} async-done(((bf16[8,112,1536]{2,1,0:T(8,128)(2,1)}), bf16[8,112,1536]{2,1,0:T(8,128)(2,1)}, u32[]{:S(2)}, u32[]{:S(2)}) %all-to-all-start.2) | async-done | bytes 2752544 | tf_op jit(solution)/shard_map/all_to_all | solution.py:105
  238.0 7.0 %all-to-all-start.1 = ((bf16[8,112,1536]{2,1,0:T(8,128)(2,1)}), bf16[8,112,1536]{2,1,0:T(8,128)(2,1)}, u32[]{:S(2)}, u32[]{:S(2)}) async-start(bf16[8,112,1536]{2,1,0:T(8,128)(2,1)} %bitcast.58), calls=%async_computation.1 | async-start | bytes 5505024 | tf_op jit(solution)/shard_map/all_to_all | solution.py:105
  245.1 0.0 copy-done
  245.1 2.9 fusion.12
  248.0 0.4 convert_reduce_fusion
  248.4 3.1 convert_reduce_fusion.1
  251.4 0.0 copy-start.1
  251.4 3.2 convert_reduce_fusion.2
  254.6 29.8 %all-to-all-done.1 = bf16[8,112,1536]{2,1,0:T(8,128)(2,1)} async-done(((bf16[8,112,1536]{2,1,0:T(8,128)(2,1)}), bf16[8,112,1536]{2,1,0:T(8,128)(2,1)}, u32[]{:S(2)}, u32[]{:S(2)}) %all-to-all-start.1) | async-done | bytes 2752544 | tf_op jit(solution)/shard_map/all_to_all | solution.py:105
  284.4 0.0 copy-start.2
  284.4 0.0 copy-start.3
  284.4 2.4 convert_reduce_fusion.3
  286.8 0.0 copy-done.1
  286.8 0.2 copy-done.2
  287.0 0.1 copy-done.3
  287.2 2.0 fusion.11
  289.2 0.1 collective-permute-start
  289.3 1.1 collective-permute-start.1
  290.4 0.1 collective-permute-start.2
  290.5 2.1 collective-permute-start.3
  292.5 9.2 %collective-permute-done = f32[112,1536]{1,0:T(8,128)S(1)} collective-permute-done((f32[112,1536]{1,0:T(8,128)S(1)}, f32[112,1536]{1,0:T(8,128)S(1)}, u32[]{:S(2)}, u32[]{:S(2)}) %collective-permute-start) | collective-permute-done | bytes 688160 | tf_op jit(solution)/shard_map/ppermute | solution.py:19
  301.7 7.4 %collective-permute-done.1 = f32[112,1536]{1,0:T(8,128)S(1)} collective-permute-done((f32[112,1536]{1,0:T(8,128)S(1)}, f32[112,1536]{1,0:T(8,128)S(1)}, u32[]{:S(2)}, u32[]{:S(2)}) %collective-permute-start.1) | collective-permute-done | bytes 688160 | tf_op jit(solution)/shard_map/ppermute | solution.py:19
  309.1 7.4 %collective-permute-done.2 = f32[112,1536]{1,0:T(8,128)S(1)} collective-permute-done((f32[112,1536]{1,0:T(8,128)S(1)}, f32[112,1536]{1,0:T(8,128)S(1)}, u32[]{:S(2)}, u32[]{:S(2)}) %collective-permute-start.2) | collective-permute-done | bytes 688160 | tf_op jit(solution)/shard_map/ppermute | solution.py:19
  316.5 7.4 %collective-permute-done.3 = f32[112,1536]{1,0:T(8,128)S(1)} collective-permute-done((f32[112,1536]{1,0:T(8,128)S(1)}, f32[112,1536]{1,0:T(8,128)S(1)}, u32[]{:S(2)}, u32[]{:S(2)}) %collective-permute-start.3) | collective-permute-done | bytes 688160 | tf_op jit(solution)/shard_map/ppermute | solution.py:19
  323.8 1.7 maximum_bitcast_fusion
  (3 shorter events, 0.0 us)
Async XLA Ops:
  0.0 245.1 %copy-start = (f32[1,2,6144]{2,1,0:T(2,128)S(1)}, f32[1,2,6144]{2,1,0:T(2,128)}, u32[]{:S(2)}) copy-start(f32[1,2,6144]{2,1,0:T(2,128)} %param.12) | copy-start | bytes 147460
  18.7 68.3 %all-to-all-start = ((bf16[8,112,2304]{2,1,0:T(8,128)(2,1)}), bf16[8,112,2304]{2,1,0:T(8,128)(2,1)}, u32[]{:S(2)}, u32[]{:S(2)}) async-start(bf16[8,112,2304]{2,1,0:T(8,128)(2,1)} %copy.13), calls=%async_computation | async-start | bytes 8257536 | tf_op jit(solution)/shard_map/all_to_all | solution.py:90
  119.4 39.8 %all-to-all-start.4 = ((bf16[8,112,1536]{2,1,0:T(8,128)(2,1)}), bf16[8,112,1536]{2,1,0:T(8,128)(2,1)S(1)}, u32[]{:S(2)}, u32[]{:S(2)}) async-start(bf16[8,112,1536]{2,1,0:T(8,128)(2,1)} %bitcast.61), calls=%async_computation.4 | async-start | bytes 5505024 | tf_op jit(solution)/shard_map/all_to_all | solution.py:105
  159.2 40.7 %all-to-all-start.3 = ((bf16[8,112,1536]{2,1,0:T(8,128)(2,1)}), bf16[8,112,1536]{2,1,0:T(8,128)(2,1)}, u32[]{:S(2)}, u32[]{:S(2)}) async-start(bf16[8,112,1536]{2,1,0:T(8,128)(2,1)} %bitcast.60), calls=%async_computation.3 | async-start | bytes 5505024 | tf_op jit(solution)/shard_map/all_to_all | solution.py:105
  199.8 38.2 %all-to-all-start.2 = ((bf16[8,112,1536]{2,1,0:T(8,128)(2,1)}), bf16[8,112,1536]{2,1,0:T(8,128)(2,1)}, u32[]{:S(2)}, u32[]{:S(2)}) async-start(bf16[8,112,1536]{2,1,0:T(8,128)(2,1)} %bitcast.59), calls=%async_computation.2 | async-start | bytes 5505024 | tf_op jit(solution)/shard_map/all_to_all | solution.py:105
  238.0 46.4 %all-to-all-start.1 = ((bf16[8,112,1536]{2,1,0:T(8,128)(2,1)}), bf16[8,112,1536]{2,1,0:T(8,128)(2,1)}, u32[]{:S(2)}, u32[]{:S(2)}) async-start(bf16[8,112,1536]{2,1,0:T(8,128)(2,1)} %bitcast.58), calls=%async_computation.1 | async-start | bytes 5505024 | tf_op jit(solution)/shard_map/all_to_all | solution.py:105
  251.4 35.4 %copy-start.1 = (f32[112,6144]{1,0:T(8,128)S(1)}, f32[112,6144]{1,0:T(8,128)}, u32[]{:S(2)}) copy-start(f32[112,6144]{1,0:T(8,128)} %fusion.12) | copy-start | bytes 8257540
  284.4 2.6 copy-start.2
  284.4 2.8 copy-start.3
  289.2 12.5 %collective-permute-start = (f32[112,1536]{1,0:T(8,128)S(1)}, f32[112,1536]{1,0:T(8,128)S(1)}, u32[]{:S(2)}, u32[]{:S(2)}) collective-permute-start(f32[112,1536]{1,0:T(8,128)S(1)} %get-tuple-element.5), channel_id=1, source_target_pairs={{0,8},{8,16},{16,24},{24,32},{32,40},{40,48},{48,56},{56,64},{64,7... | collective-permute-start | bytes 2064392 | tf_op jit(solution)/shard_map/ppermute | solution.py:19
  289.3 19.8 %collective-permute-start.1 = (f32[112,1536]{1,0:T(8,128)S(1)}, f32[112,1536]{1,0:T(8,128)S(1)}, u32[]{:S(2)}, u32[]{:S(2)}) collective-permute-start(f32[112,1536]{1,0:T(8,128)S(1)} %get-tuple-element.8), channel_id=1, source_target_pairs={{0,8},{8,16},{16,24},{24,32},{32,40},{40,48},{48,56},{56,64},{64,7... | collective-permute-start | bytes 2064392 | tf_op jit(solution)/shard_map/ppermute | solution.py:19
  290.4 26.1 %collective-permute-start.2 = (f32[112,1536]{1,0:T(8,128)S(1)}, f32[112,1536]{1,0:T(8,128)S(1)}, u32[]{:S(2)}, u32[]{:S(2)}) collective-permute-start(f32[112,1536]{1,0:T(8,128)S(1)} %get-tuple-element.7), channel_id=1, source_target_pairs={{0,8},{8,16},{16,24},{24,32},{32,40},{40,48},{48,56},{56,64},{64,7... | collective-permute-start | bytes 2064392 | tf_op jit(solution)/shard_map/ppermute | solution.py:19
  290.5 33.4 %collective-permute-start.3 = (f32[112,1536]{1,0:T(8,128)S(1)}, f32[112,1536]{1,0:T(8,128)S(1)}, u32[]{:S(2)}, u32[]{:S(2)}) collective-permute-start(f32[112,1536]{1,0:T(8,128)S(1)} %get-tuple-element.6), channel_id=1, source_target_pairs={{0,8},{8,16},{16,24},{24,32},{32,40},{40,48},{48,56},{56,64},{64,7... | collective-permute-start | bytes 2064392 | tf_op jit(solution)/shard_map/ppermute | solution.py:19

commit v7 on v6

--- a/solution.py
+++ b/solution.py
@@ -95,7 +95,7 @@
     picker = (video_of[:, None] == jnp.arange(VIDS, dtype=jnp.int32)[None, :]).astype(jnp.float32)
     gains = jnp.dot(picker, gate[0], precision=lax.Precision.HIGHEST)
     width = out_proj.shape[2]
-    pieces = 4
+    pieces = 2
     step = width // pieces
     outs = []
     for c in range(pieces):

time: 326 us -> 328 us (level)
  waiting for transfers between devices: 198 us -> 225 us
  starting transfers between devices: 39.3 us -> 23.4 us
  matrix products: 26.6 us -> 19.4 us
    all_to_all x4 -> x2, waiting for transfers between devices: 110 us -> 135 us  [per_device(): shares = lax.all_to_all(shares, 'sp', 0, 0, tiled=True)]
    all_to_all x4 -> x2, starting transfers between devices: 27.9 us -> 14 us  [per_device(): shares = lax.all_to_all(shares, 'sp', 0, 0, tiled=True)]
    dot_general x4 -> x2, matrix products: 23.7 us -> 18.2 us  [per_device(): jnp.dot(heads_all, out_proj[0, :, cols], preferred_element_type=jnp.float32)]
    ppermute x4 -> x2, waiting for transfers between devices: 31.3 us -> 33.3 us  [passed_along(): lax.ppermute(shard, axis, [(i, (i + by) % devices) for i in range(devices)])]
    reduce_sum x4 -> x2, other arithmetic: 9.04 us -> 8.55 us  [per_device(): projected = jnp.sum(shares.astype(jnp.float32), axis=0)]
  transfers between devices with their start and end apart: 9 -> 5, of which waited for: 9 -> 5; matrix products, arithmetic and copies ran while one was open for 9% -> 5% of each run, Pallas kernels for 0% -> 0%
where the time goes in v7:
time: 328 us; the launch traced here: 327 us
  waiting for transfers between devices  225 us (69%)
  Pallas kernels  26.3 us (8%)
  starting transfers between devices  23.4 us (7%)
  local copies, waits for them, and re-layouts  20.2 us (6%)
  matrix products  19.4 us (6%)
  other arithmetic  11.1 us (3%)
    all_to_all x2, waiting for transfers between devices, per_device(): shares = lax.all_to_all(shares, 'sp', 0, 0, tiled=True)  135 us
    all_to_all x1, waiting for transfers between devices, per_device(): spread = lax.all_to_all(grouped, 'sp', 0, 0, tiled=True)  57.3 us
    ppermute x2, waiting for transfers between devices, passed_along(): lax.ppermute(shard, axis, [(i, (i + by) % devices) for i in range(devices)])  33.3 us
    pallas_call x1, Pallas kernels, attend_all(): pl.pallas_call(attend_kernel, grid=(VIDS,), in_specs=[pl.BlockSpec((1, KE...  26.3 us
    dot_general x2, matrix products, per_device(): jnp.dot(heads_all, out_proj[0, :, cols], preferred_element_type=jnp.float32)  18.2 us
    all_to_all x2, starting transfers between devices, per_device(): shares = lax.all_to_all(shares, 'sp', 0, 0, tiled=True)  14 us
    reduce_sum x2, other arithmetic, per_device(): projected = jnp.sum(shares.astype(jnp.float32), axis=0)  8.55 us
    all_to_all x1, starting transfers between devices, per_device(): spread = lax.all_to_all(grouped, 'sp', 0, 0, tiled=True)  8.09 us
  transfers between devices with their start and end apart: 5, of which 5 were waited for; matrix products, arithmetic and copies ran while one was open for 5% of the time, Pallas kernels for 0%

profile of v7, /device:TPU:6, one launch (start us, length us, event | category | flops | bytes accessed | tf_op | source)
XLA Modules:
  0.0 327.1 jit_solution(15864815286685859346)
XLA Ops:
  0.0 0.0 copy-start
  0.0 5.4 %copy.14 = bf16[42,8,8,768]{3,2,1,0:T(8,128)(2,1)} copy(bf16[42,8,8,768]{3,1,2,0:T(8,128)(2,1)} %bitcast.45) | data formatting | bytes 8257536
  5.4 6.8 %copy.12 = bf16[112,3,8,768]{0,3,1,2:T(8,128)(2,1)} copy(bf16[112,3,8,768]{3,2,0,1:T(8,128)(2,1)} %bitcast.42) | data formatting | bytes 8257536 | tf_op jit(solution)/shard_map/reshape;squeeze | solution.py:88
  12.2 6.5 %copy.13 = bf16[8,112,2304]{2,1,0:T(8,128)(2,1)} copy(bf16[8,112,2304]{1,2,0:T(8,128)(2,1)} %bitcast.41) | data formatting | bytes 8257536 | tf_op jit(solution)/shard_map/reshape | solution.py:89
  18.7 8.1 %all-to-all-start = ((bf16[8,112,2304]{2,1,0:T(8,128)(2,1)}), bf16[8,112,2304]{2,1,0:T(8,128)(2,1)}, u32[]{:S(2)}, u32[]{:S(2)}) async-start(bf16[8,112,2304]{2,1,0:T(8,128)(2,1)} %copy.13), calls=%async_computation | async-start | bytes 8257536 | tf_op jit(solution)/shard_map/all_to_all | solution.py:90
  28.1 0.7 dynamic-slice_bitcast_fusion
  28.8 0.2 select_reduce_fusion
  29.0 0.1 broadcast_in_dim.38
  29.1 0.7 broadcast_in_dim_reshape.3.bias_ref
  29.8 57.3 %all-to-all-done.own_ref = bf16[8,112,2304]{2,1,0:T(8,128)(2,1)} async-done(((bf16[8,112,2304]{2,1,0:T(8,128)(2,1)}), bf16[8,112,2304]{2,1,0:T(8,128)(2,1)}, u32[]{:S(2)}, u32[]{:S(2)}) %all-to-all-start) | async-done | bytes 4128800 | tf_op jit(solution)/shard_map/all_to_all | solution.py:90
  87.0 26.3 %shard_map.82 = bf16[896,768]{1,0:T(8,128)(2,1)} custom-call(f32[1,1344]{1,0:T(1,128)} %broadcast_in_dim_reshape.3.bias_ref, bf16[8,112,2304]{2,1,0:T(8,128)(2,1)} %all-to-all-done.own_ref, bf16[2,2,1344,768]{3,2,1,0:T(8,128)(2,1)} %bitcast.39, bf16[2,2,1344,768]{3,2,1,0:T(8,128)(2,1)} %bitcast.40), custom_call_target="tpu_custom_call" | custom-call | tf_op jit(solution)/shard_map/pallas_call | solution.py:65
  113.4 9.6 %convolution_convert_fusion = bf16[896,3072]{1,0:T(8,128)(2,1)} fusion(bf16[896,768]{1,0:T(8,128)(2,1)} %shard_map.82, bf16[1,768,6144]{2,1,0:T(8,128)(2,1)} %param.11), kind=kOutput, calls=%fused_computation.2 | convolution fusion | flops 4230610944 | bytes 11599872 | tf_op jit(solution)/shard_map/dot_general | solution.py:103
  123.0 0.0 copy-start.3
  123.0 7.0 %all-to-all-start.2 = ((bf16[8,112,3072]{2,1,0:T(8,128)(2,1)}), bf16[8,112,3072]{2,1,0:T(8,128)(2,1)}, u32[]{:S(2)}, u32[]{:S(2)}) async-start(bf16[8,112,3072]{2,1,0:T(8,128)(2,1)} %bitcast.44), calls=%async_computation.2 | async-start | bytes 11010048 | tf_op jit(solution)/shard_map/all_to_all | solution.py:105
  130.0 0.0 copy-done.3
  130.0 8.6 %convolution_convert_fusion.1 = bf16[896,3072]{1,0:T(8,128)(2,1)} fusion(bf16[896,768]{1,0:T(8,128)(2,1)S(1)} %copy-done.3, bf16[1,768,6144]{2,1,0:T(8,128)(2,1)} %param.11), kind=kOutput, calls=%fused_computation.3 | convolution fusion | flops 4230610944 | bytes 11599872 | tf_op jit(solution)/shard_map/dot_general | solution.py:103
  138.6 68.9 %all-to-all-done.2 = bf16[8,112,3072]{2,1,0:T(8,128)(2,1)} async-done(((bf16[8,112,3072]{2,1,0:T(8,128)(2,1)}), bf16[8,112,3072]{2,1,0:T(8,128)(2,1)}, u32[]{:S(2)}, u32[]{:S(2)}) %all-to-all-start.2) | async-done | bytes 5505056 | tf_op jit(solution)/shard_map/all_to_all | solution.py:105
  207.6 6.9 %all-to-all-start.1 = ((bf16[8,112,3072]{2,1,0:T(8,128)(2,1)}), bf16[8,112,3072]{2,1,0:T(8,128)(2,1)}, u32[]{:S(2)}, u32[]{:S(2)}) async-start(bf16[8,112,3072]{2,1,0:T(8,128)(2,1)} %bitcast.43), calls=%async_computation.1 | async-start | bytes 11010048 | tf_op jit(solution)/shard_map/all_to_all | solution.py:105
  214.5 0.0 copy-done
  214.5 1.3 fusion.6
  215.8 4.7 %convert_reduce_fusion = f32[112,3072]{1,0:T(8,128)} fusion(bf16[8,112,3072]{2,1,0:T(8,128)(2,1)} %all-to-all-done.2), kind=kLoop, calls=%fused_computation | loop fusion | flops 5160960 | bytes 6881280 | tf_op jit(solution)/shard_map/reduce_sum | solution.py:106
  220.5 65.8 %all-to-all-done.1 = bf16[8,112,3072]{2,1,0:T(8,128)(2,1)} async-done(((bf16[8,112,3072]{2,1,0:T(8,128)(2,1)}), bf16[8,112,3072]{2,1,0:T(8,128)(2,1)}, u32[]{:S(2)}, u32[]{:S(2)}) %all-to-all-start.1) | async-done | bytes 5505056 | tf_op jit(solution)/shard_map/all_to_all | solution.py:105
  286.2 0.0 copy-start.1
  286.2 0.0 copy-start.2
  286.2 3.8 %convert_reduce_fusion.1 = f32[112,3072]{1,0:T(8,128)S(1)} fusion(bf16[8,112,3072]{2,1,0:T(8,128)(2,1)} %all-to-all-done.1), kind=kLoop, calls=%fused_computation.1 | loop fusion | flops 5160960 | bytes 6881280 | tf_op jit(solution)/shard_map/reduce_sum | solution.py:106
  290.1 0.0 copy-done.1
  290.1 0.0 copy-done.2
  290.1 0.6 fusion.5
  290.7 0.1 collective-permute-start
  290.8 1.3 collective-permute-start.1
  292.1 18.6 %collective-permute-done = f32[112,3072]{1,0:T(8,128)S(1)} collective-permute-done((f32[112,3072]{1,0:T(8,128)S(1)}, f32[112,3072]{1,0:T(8,128)S(1)}, u32[]{:S(2)}, u32[]{:S(2)}) %collective-permute-start) | collective-permute-done | bytes 1376288 | tf_op jit(solution)/shard_map/ppermute | solution.py:19
  310.6 14.7 %collective-permute-done.1 = f32[112,3072]{1,0:T(8,128)S(1)} collective-permute-done((f32[112,3072]{1,0:T(8,128)S(1)}, f32[112,3072]{1,0:T(8,128)S(1)}, u32[]{:S(2)}, u32[]{:S(2)}) %collective-permute-start.1) | collective-permute-done | bytes 1376288 | tf_op jit(solution)/shard_map/ppermute | solution.py:19
  325.4 1.7 maximum_bitcast_fusion
  (3 shorter events, 0.0 us)
Async XLA Ops:
  0.0 214.5 %copy-start = (f32[1,2,6144]{2,1,0:T(2,128)S(1)}, f32[1,2,6144]{2,1,0:T(2,128)}, u32[]{:S(2)}) copy-start(f32[1,2,6144]{2,1,0:T(2,128)} %param.12) | copy-start | bytes 147460
  18.7 68.3 %all-to-all-start = ((bf16[8,112,2304]{2,1,0:T(8,128)(2,1)}), bf16[8,112,2304]{2,1,0:T(8,128)(2,1)}, u32[]{:S(2)}, u32[]{:S(2)}) async-start(bf16[8,112,2304]{2,1,0:T(8,128)(2,1)} %copy.13), calls=%async_computation | async-start | bytes 8257536 | tf_op jit(solution)/shard_map/all_to_all | solution.py:90
  123.0 7.1 %copy-start.3 = (bf16[896,768]{1,0:T(8,128)(2,1)S(1)}, bf16[896,768]{1,0:T(8,128)(2,1)}, u32[]{:S(2)}) copy-start(bf16[896,768]{1,0:T(8,128)(2,1)} %shard_map.82) | copy-start | bytes 4128772
  123.0 84.6 %all-to-all-start.2 = ((bf16[8,112,3072]{2,1,0:T(8,128)(2,1)}), bf16[8,112,3072]{2,1,0:T(8,128)(2,1)}, u32[]{:S(2)}, u32[]{:S(2)}) async-start(bf16[8,112,3072]{2,1,0:T(8,128)(2,1)} %bitcast.44), calls=%async_computation.2 | async-start | bytes 11010048 | tf_op jit(solution)/shard_map/all_to_all | solution.py:105
  207.6 78.7 %all-to-all-start.1 = ((bf16[8,112,3072]{2,1,0:T(8,128)(2,1)}), bf16[8,112,3072]{2,1,0:T(8,128)(2,1)}, u32[]{:S(2)}, u32[]{:S(2)}) async-start(bf16[8,112,3072]{2,1,0:T(8,128)(2,1)} %bitcast.43), calls=%async_computation.1 | async-start | bytes 11010048 | tf_op jit(solution)/shard_map/all_to_all | solution.py:105
  286.2 3.9 %copy-start.1 = (f32[112,3072]{1,0:T(8,128)S(1)}, f32[112,3072]{1,0:T(8,128)}, u32[]{:S(2)}) copy-start(f32[112,3072]{1,0:T(8,128)} %convert_reduce_fusion) | copy-start | bytes 4128772
  286.2 3.9 %copy-start.2 = (f32[1,112,6144]{2,1,0:T(8,128)S(1)}, f32[1,112,6144]{2,1,0:T(8,128)}, u32[]{:S(2)}) copy-start(f32[1,112,6144]{2,1,0:T(8,128)} %param.8) | copy-start | bytes 8257540
  290.7 19.9 %collective-permute-start = (f32[112,3072]{1,0:T(8,128)S(1)}, f32[112,3072]{1,0:T(8,128)S(1)}, u32[]{:S(2)}, u32[]{:S(2)}) collective-permute-start(f32[112,3072]{1,0:T(8,128)S(1)} %get-tuple-element.5), channel_id=1, source_target_pairs={{0,8},{8,16},{16,24},{24,32},{32,40},{40,48},{48,56},{56,64},{64,7... | collective-permute-start | bytes 4128776 | tf_op jit(solution)/shard_map/ppermute | solution.py:19
  290.8 34.6 %collective-permute-start.1 = (f32[112,3072]{1,0:T(8,128)S(1)}, f32[112,3072]{1,0:T(8,128)S(1)}, u32[]{:S(2)}, u32[]{:S(2)}) collective-permute-start(f32[112,3072]{1,0:T(8,128)S(1)} %get-tuple-element.6), channel_id=1, source_target_pairs={{0,8},{8,16},{16,24},{24,32},{32,40},{40,48},{48,56},{56,64},{64,7... | collective-permute-start | bytes 4128776 | tf_op jit(solution)/shard_map/ppermute | solution.py:19

commit v8 on v5

--- a/solution.py
+++ b/solution.py
@@ -48,8 +48,9 @@
         far_raised = jnp.exp(far - highest)
         near_raised = jnp.exp(near - highest)
         total = jnp.sum(far_raised, axis=1, keepdims=True) + jnp.sum(near_raised, axis=1, keepdims=True)
-        far_w = (far_raised / total).astype(jnp.bfloat16)
-        near_w = (near_raised / total).astype(jnp.bfloat16)
+        inverse = 1.0 / total
+        far_w = (far_raised * inverse).astype(jnp.bfloat16)
+        near_w = (near_raised * inverse).astype(jnp.bfloat16)
         mixed = jnp.dot(far_w, vc, preferred_element_type=jnp.float32) + jnp.dot(
             near_w, vn, preferred_element_type=jnp.float32
         )

time: 320 us -> 320 us (level)
  no operation moved by 1% of the time
where the time goes in v8:
time: 320 us; the launch traced here: 319 us
  waiting for transfers between devices  206 us (64%)
  starting transfers between devices  30.1 us (9%)
  Pallas kernels  26.3 us (8%)
  matrix products  21.1 us (7%)
  local copies, waits for them, and re-layouts  20.7 us (6%)
  other arithmetic  13.1 us (4%)
    all_to_all x3, waiting for transfers between devices, per_device(): shares = lax.all_to_all(shares, 'sp', 0, 0, tiled=True)  115 us
    all_to_all x1, waiting for transfers between devices, per_device(): spread = lax.all_to_all(grouped, 'sp', 0, 0, tiled=True)  57.3 us
    ppermute x3, waiting for transfers between devices, passed_along(): lax.ppermute(shard, axis, [(i, (i + by) % devices) for i in range(devices)])  33.5 us
    pallas_call x1, Pallas kernels, attend_all(): pl.pallas_call(attend_kernel, grid=(VIDS,), in_specs=[pl.BlockSpec((1, KE...  26.3 us
    all_to_all x3, starting transfers between devices, per_device(): shares = lax.all_to_all(shares, 'sp', 0, 0, tiled=True)  20.9 us
    dot_general x3, matrix products, per_device(): jnp.dot(heads_all, out_proj[0, :, cols], preferred_element_type=jnp.float32)  19.8 us
    reduce_sum x3, other arithmetic, per_device(): projected = jnp.sum(shares.astype(jnp.float32), axis=0)  10.4 us
    all_to_all x1, starting transfers between devices, per_device(): spread = lax.all_to_all(grouped, 'sp', 0, 0, tiled=True)  8.09 us
  transfers between devices with their start and end apart: 7, of which 7 were waited for; matrix products, arithmetic and copies ran while one was open for 7% of the time, Pallas kernels for 0%

profile of v8, /device:TPU:6, one launch (start us, length us, event | category | flops | bytes accessed | tf_op | source)
XLA Modules:
  0.0 318.9 jit_solution(14387522826098219809)
XLA Ops:
  0.0 0.0 copy-start
  0.0 5.4 %copy.14 = bf16[42,8,8,768]{3,2,1,0:T(8,128)(2,1)} copy(bf16[42,8,8,768]{3,1,2,0:T(8,128)(2,1)} %bitcast.50) | data formatting | bytes 8257536
  5.4 6.7 %copy.12 = bf16[112,3,8,768]{0,3,1,2:T(8,128)(2,1)} copy(bf16[112,3,8,768]{3,2,0,1:T(8,128)(2,1)} %bitcast.49) | data formatting | bytes 8257536 | tf_op jit(solution)/shard_map/reshape;squeeze | solution.py:89
  12.2 6.6 %copy.13 = bf16[8,112,2304]{2,1,0:T(8,128)(2,1)} copy(bf16[8,112,2304]{1,2,0:T(8,128)(2,1)} %bitcast.48) | data formatting | bytes 8257536 | tf_op jit(solution)/shard_map/reshape | solution.py:90
  18.7 8.1 %all-to-all-start = ((bf16[8,112,2304]{2,1,0:T(8,128)(2,1)}), bf16[8,112,2304]{2,1,0:T(8,128)(2,1)}, u32[]{:S(2)}, u32[]{:S(2)}) async-start(bf16[8,112,2304]{2,1,0:T(8,128)(2,1)} %copy.13), calls=%async_computation | async-start | bytes 8257536 | tf_op jit(solution)/shard_map/all_to_all | solution.py:91
  28.2 0.7 dynamic-slice_bitcast_fusion
  28.9 0.2 select_reduce_fusion
  29.0 0.1 broadcast_in_dim.38
  29.1 0.7 broadcast_in_dim_reshape.3.bias_ref
  29.8 57.3 %all-to-all-done.own_ref = bf16[8,112,2304]{2,1,0:T(8,128)(2,1)} async-done(((bf16[8,112,2304]{2,1,0:T(8,128)(2,1)}), bf16[8,112,2304]{2,1,0:T(8,128)(2,1)}, u32[]{:S(2)}, u32[]{:S(2)}) %all-to-all-start) | async-done | bytes 4128800 | tf_op jit(solution)/shard_map/all_to_all | solution.py:91
  87.1 26.3 %shard_map.82 = bf16[896,768]{1,0:T(8,128)(2,1)} custom-call(f32[1,1344]{1,0:T(1,128)} %broadcast_in_dim_reshape.3.bias_ref, bf16[8,112,2304]{2,1,0:T(8,128)(2,1)} %all-to-all-done.own_ref, bf16[2,2,1344,768]{3,2,1,0:T(8,128)(2,1)} %bitcast.46, bf16[2,2,1344,768]{3,2,1,0:T(8,128)(2,1)} %bitcast.47), custom_call_target="tpu_custom_call" | custom-call | tf_op jit(solution)/shard_map/pallas_call | solution.py:66
  113.4 7.2 %convolution_convert_fusion = bf16[896,2048]{1,0:T(8,128)(2,1)} fusion(bf16[896,768]{1,0:T(8,128)(2,1)} %shard_map.82, bf16[1,768,6144]{2,1,0:T(8,128)(2,1)} %param.11), kind=kOutput, calls=%fused_computation.3 | convolution fusion | flops 2820407296 | bytes 8192000 | tf_op jit(solution)/shard_map/dot_general | solution.py:104
  120.6 0.0 copy-start.4
  120.6 7.0 %all-to-all-start.3 = ((bf16[8,112,2048]{2,1,0:T(8,128)(2,1)}), bf16[8,112,2048]{2,1,0:T(8,128)(2,1)}, u32[]{:S(2)}, u32[]{:S(2)}) async-start(bf16[8,112,2048]{2,1,0:T(8,128)(2,1)} %bitcast.53), calls=%async_computation.3 | async-start | bytes 7340032 | tf_op jit(solution)/shard_map/all_to_all | solution.py:106
  127.6 0.0 copy-done.4
  127.6 6.3 %convolution_convert_fusion.1 = bf16[896,2048]{1,0:T(8,128)(2,1)} fusion(bf16[896,768]{1,0:T(8,128)(2,1)S(1)} %copy-done.4, bf16[1,768,6144]{2,1,0:T(8,128)(2,1)} %param.11), kind=kOutput, calls=%fused_computation.4 | convolution fusion | flops 2820407296 | bytes 8192000 | tf_op jit(solution)/shard_map/dot_general | solution.py:104
  134.0 41.6 %all-to-all-done.3 = bf16[8,112,2048]{2,1,0:T(8,128)(2,1)} async-done(((bf16[8,112,2048]{2,1,0:T(8,128)(2,1)}), bf16[8,112,2048]{2,1,0:T(8,128)(2,1)}, u32[]{:S(2)}, u32[]{:S(2)}) %all-to-all-start.3) | async-done | bytes 3670048 | tf_op jit(solution)/shard_map/all_to_all | solution.py:106
  175.6 6.9 %all-to-all-start.2 = ((bf16[8,112,2048]{2,1,0:T(8,128)(2,1)}), bf16[8,112,2048]{2,1,0:T(8,128)(2,1)}, u32[]{:S(2)}, u32[]{:S(2)}) async-start(bf16[8,112,2048]{2,1,0:T(8,128)(2,1)} %bitcast.52), calls=%async_computation.2 | async-start | bytes 7340032 | tf_op jit(solution)/shard_map/all_to_all | solution.py:106
  182.5 6.3 %convolution_convert_fusion.2 = bf16[896,2048]{1,0:T(8,128)(2,1)} fusion(bf16[896,768]{1,0:T(8,128)(2,1)S(1)} %copy-done.4, bf16[1,768,6144]{2,1,0:T(8,128)(2,1)} %param.11), kind=kOutput, calls=%fused_computation.5 | convolution fusion | flops 2820407296 | bytes 8192000 | tf_op jit(solution)/shard_map/dot_general | solution.py:104
  188.8 35.7 %all-to-all-done.2 = bf16[8,112,2048]{2,1,0:T(8,128)(2,1)} async-done(((bf16[8,112,2048]{2,1,0:T(8,128)(2,1)}), bf16[8,112,2048]{2,1,0:T(8,128)(2,1)}, u32[]{:S(2)}, u32[]{:S(2)}) %all-to-all-start.2) | async-done | bytes 3670048 | tf_op jit(solution)/shard_map/all_to_all | solution.py:106
  224.5 6.9 %all-to-all-start.1 = ((bf16[8,112,2048]{2,1,0:T(8,128)(2,1)}), bf16[8,112,2048]{2,1,0:T(8,128)(2,1)}, u32[]{:S(2)}, u32[]{:S(2)}) async-start(bf16[8,112,2048]{2,1,0:T(8,128)(2,1)} %bitcast.51), calls=%async_computation.1 | async-start | bytes 7340032 | tf_op jit(solution)/shard_map/all_to_all | solution.py:106
  231.5 0.0 copy-done
  231.5 1.3 fusion.9
  232.8 3.7 %convert_reduce_fusion = f32[112,2048]{1,0:T(8,128)} fusion(bf16[8,112,2048]{2,1,0:T(8,128)(2,1)} %all-to-all-done.3), kind=kLoop, calls=%fused_computation | loop fusion | flops 3440640 | bytes 4587520 | tf_op jit(solution)/shard_map/reduce_sum | solution.py:107
  236.5 3.7 %convert_reduce_fusion.1 = f32[112,2048]{1,0:T(8,128)} fusion(bf16[8,112,2048]{2,1,0:T(8,128)(2,1)} %all-to-all-done.2), kind=kLoop, calls=%fused_computation.1 | loop fusion | flops 3440640 | bytes 4587520 | tf_op jit(solution)/shard_map/reduce_sum | solution.py:107
  240.2 38.1 %all-to-all-done.1 = bf16[8,112,2048]{2,1,0:T(8,128)(2,1)} async-done(((bf16[8,112,2048]{2,1,0:T(8,128)(2,1)}), bf16[8,112,2048]{2,1,0:T(8,128)(2,1)}, u32[]{:S(2)}, u32[]{:S(2)}) %all-to-all-start.1) | async-done | bytes 3670048 | tf_op jit(solution)/shard_map/all_to_all | solution.py:106
  278.3 0.0 copy-start.1
  278.3 0.0 copy-start.2
  278.3 0.0 copy-start.3
  278.3 3.0 convert_reduce_fusion.2
  281.2 0.0 copy-done.1
  281.2 0.0 copy-done.2
  281.3 0.4 copy-done.3
  281.7 0.8 fusion.8
  282.5 0.1 collective-permute-start
  282.6 1.0 collective-permute-start.1
  283.6 0.1 collective-permute-start.2
  283.7 13.8 %collective-permute-done = f32[112,2048]{1,0:T(8,128)S(1)} collective-permute-done((f32[112,2048]{1,0:T(8,128)S(1)}, f32[112,2048]{1,0:T(8,128)S(1)}, u32[]{:S(2)}, u32[]{:S(2)}) %collective-permute-start) | collective-permute-done | bytes 917536 | tf_op jit(solution)/shard_map/ppermute | solution.py:19
  297.5 9.8 %collective-permute-done.1 = f32[112,2048]{1,0:T(8,128)S(1)} collective-permute-done((f32[112,2048]{1,0:T(8,128)S(1)}, f32[112,2048]{1,0:T(8,128)S(1)}, u32[]{:S(2)}, u32[]{:S(2)}) %collective-permute-start.1) | collective-permute-done | bytes 917536 | tf_op jit(solution)/shard_map/ppermute | solution.py:19
  307.3 9.8 %collective-permute-done.2 = f32[112,2048]{1,0:T(8,128)S(1)} collective-permute-done((f32[112,2048]{1,0:T(8,128)S(1)}, f32[112,2048]{1,0:T(8,128)S(1)}, u32[]{:S(2)}, u32[]{:S(2)}) %collective-permute-start.2) | collective-permute-done | bytes 917536 | tf_op jit(solution)/shard_map/ppermute | solution.py:19
  317.2 1.7 maximum_bitcast_fusion
  (3 shorter events, 0.0 us)
Async XLA Ops:
  0.0 231.5 %copy-start = (f32[1,2,6144]{2,1,0:T(2,128)S(1)}, f32[1,2,6144]{2,1,0:T(2,128)}, u32[]{:S(2)}) copy-start(f32[1,2,6144]{2,1,0:T(2,128)} %param.12) | copy-start | bytes 147460
  18.7 68.3 %all-to-all-start = ((bf16[8,112,2304]{2,1,0:T(8,128)(2,1)}), bf16[8,112,2304]{2,1,0:T(8,128)(2,1)}, u32[]{:S(2)}, u32[]{:S(2)}) async-start(bf16[8,112,2304]{2,1,0:T(8,128)(2,1)} %copy.13), calls=%async_computation | async-start | bytes 8257536 | tf_op jit(solution)/shard_map/all_to_all | solution.py:91
  120.6 7.1 %copy-start.4 = (bf16[896,768]{1,0:T(8,128)(2,1)S(1)}, bf16[896,768]{1,0:T(8,128)(2,1)}, u32[]{:S(2)}) copy-start(bf16[896,768]{1,0:T(8,128)(2,1)} %shard_map.82) | copy-start | bytes 4128772
  120.6 55.0 %all-to-all-start.3 = ((bf16[8,112,2048]{2,1,0:T(8,128)(2,1)}), bf16[8,112,2048]{2,1,0:T(8,128)(2,1)}, u32[]{:S(2)}, u32[]{:S(2)}) async-start(bf16[8,112,2048]{2,1,0:T(8,128)(2,1)} %bitcast.53), calls=%async_computation.3 | async-start | bytes 7340032 | tf_op jit(solution)/shard_map/all_to_all | solution.py:106
  175.6 49.0 %all-to-all-start.2 = ((bf16[8,112,2048]{2,1,0:T(8,128)(2,1)}), bf16[8,112,2048]{2,1,0:T(8,128)(2,1)}, u32[]{:S(2)}, u32[]{:S(2)}) async-start(bf16[8,112,2048]{2,1,0:T(8,128)(2,1)} %bitcast.52), calls=%async_computation.2 | async-start | bytes 7340032 | tf_op jit(solution)/shard_map/all_to_all | solution.py:106
  224.5 53.7 %all-to-all-start.1 = ((bf16[8,112,2048]{2,1,0:T(8,128)(2,1)}), bf16[8,112,2048]{2,1,0:T(8,128)(2,1)}, u32[]{:S(2)}, u32[]{:S(2)}) async-start(bf16[8,112,2048]{2,1,0:T(8,128)(2,1)} %bitcast.51), calls=%async_computation.1 | async-start | bytes 7340032 | tf_op jit(solution)/shard_map/all_to_all | solution.py:106
  278.3 3.0 copy-start.1
  278.3 3.0 copy-start.2
  278.3 3.4 %copy-start.3 = (f32[1,112,6144]{2,1,0:T(8,128)S(1)}, f32[1,112,6144]{2,1,0:T(8,128)}, u32[]{:S(2)}) copy-start(f32[1,112,6144]{2,1,0:T(8,128)} %param.8) | copy-start | bytes 8257540
  282.5 15.0 %collective-permute-start = (f32[112,2048]{1,0:T(8,128)S(1)}, f32[112,2048]{1,0:T(8,128)S(1)}, u32[]{:S(2)}, u32[]{:S(2)}) collective-permute-start(f32[112,2048]{1,0:T(8,128)S(1)} %get-tuple-element.5), channel_id=1, source_target_pairs={{0,8},{8,16},{16,24},{24,32},{32,40},{40,48},{48,56},{56,64},{64,7... | collective-permute-start | bytes 2752520 | tf_op jit(solution)/shard_map/ppermute | solution.py:19
  282.6 24.7 %collective-permute-start.1 = (f32[112,2048]{1,0:T(8,128)S(1)}, f32[112,2048]{1,0:T(8,128)S(1)}, u32[]{:S(2)}, u32[]{:S(2)}) collective-permute-start(f32[112,2048]{1,0:T(8,128)S(1)} %get-tuple-element.7), channel_id=1, source_target_pairs={{0,8},{8,16},{16,24},{24,32},{32,40},{40,48},{48,56},{56,64},{64,7... | collective-permute-start | bytes 2752520 | tf_op jit(solution)/shard_map/ppermute | solution.py:19
  283.6 33.6 %collective-permute-start.2 = (f32[112,2048]{1,0:T(8,128)S(1)}, f32[112,2048]{1,0:T(8,128)S(1)}, u32[]{:S(2)}, u32[]{:S(2)}) collective-permute-start(f32[112,2048]{1,0:T(8,128)S(1)} %get-tuple-element.6), channel_id=1, source_target_pairs={{0,8},{8,16},{16,24},{24,32},{32,40},{40,48},{48,56},{56,64},{64,7... | collective-permute-start | bytes 2752520 | tf_op jit(solution)/shard_map/ppermute | solution.py:19

commit v9 on v8

--- a/solution.py
+++ b/solution.py
@@ -96,11 +96,12 @@
     picker = (video_of[:, None] == jnp.arange(VIDS, dtype=jnp.int32)[None, :]).astype(jnp.float32)
     gains = jnp.dot(picker, gate[0], precision=lax.Precision.HIGHEST)
     width = out_proj.shape[2]
-    pieces = 3
-    step = width // pieces
+    unit = width // 12
+    bounds = [0, 5 * unit, 9 * unit, width]
     outs = []
-    for c in range(pieces):
-        cols = slice(c * step, (c + 1) * step)
+    for c in range(len(bounds) - 1):
+        cols = slice(bounds[c], bounds[c + 1])
+        step = bounds[c + 1] - bounds[c]
         partial = jnp.dot(heads_all, out_proj[0, :, cols], preferred_element_type=jnp.float32)
         shares = partial.astype(jnp.bfloat16).reshape(devices, own_rows, step)
         shares = lax.all_to_all(shares, "sp", 0, 0, tiled=True)

time: 320 us -> 322 us (level)
  starting transfers between devices: 30.1 us -> 42.1 us
  waiting for transfers between devices: 206 us -> 194 us
    ppermute x3, waiting for transfers between devices: 33.5 us -> 18.7 us  [passed_along(): lax.ppermute(shard, axis, [(i, (i + by) % devices) for i in range(devices)])]
    ppermute x3, starting transfers between devices: 1.15 us -> 13.2 us  [passed_along(): lax.ppermute(shard, axis, [(i, (i + by) % devices) for i in range(devices)])]
    reduce_sum x3, other arithmetic: 10.4 us -> 6.9 us  [per_device(): projected = jnp.sum(shares.astype(jnp.float32), axis=0)]
  transfers between devices with their start and end apart: 7 -> 7, of which waited for: 7 -> 5; matrix products, arithmetic and copies ran while one was open for 7% -> 9% of each run, Pallas kernels for 0% -> 0%
where the time goes in v9:
time: 322 us; the launch traced here: 319 us
  waiting for transfers between devices  194 us (60%)
  starting transfers between devices  42.1 us (13%)
  Pallas kernels  26.4 us (8%)
  matrix products  22.6 us (7%)
  local copies, waits for them, and re-layouts  20.3 us (6%)
  other arithmetic  12.6 us (4%)
    all_to_all x3, waiting for transfers between devices, per_device(): shares = lax.all_to_all(shares, 'sp', 0, 0, tiled=True)  118 us
    all_to_all x1, waiting for transfers between devices, per_device(): spread = lax.all_to_all(grouped, 'sp', 0, 0, tiled=True)  57.3 us
    pallas_call x1, Pallas kernels, attend_all(): pl.pallas_call(attend_kernel, grid=(VIDS,), in_specs=[pl.BlockSpec((1, KE...  26.4 us
    dot_general x3, matrix products, per_device(): jnp.dot(heads_all, out_proj[0, :, cols], preferred_element_type=jnp.float32)  21.4 us
    all_to_all x3, starting transfers between devices, per_device(): shares = lax.all_to_all(shares, 'sp', 0, 0, tiled=True)  20.9 us
    ppermute x3, waiting for transfers between devices, passed_along(): lax.ppermute(shard, axis, [(i, (i + by) % devices) for i in range(devices)])  18.7 us
    ppermute x3, starting transfers between devices, passed_along(): lax.ppermute(shard, axis, [(i, (i + by) % devices) for i in range(devices)])  13.2 us
    all_to_all x1, starting transfers between devices, per_device(): spread = lax.all_to_all(grouped, 'sp', 0, 0, tiled=True)  8.09 us
  transfers between devices with their start and end apart: 7, of which 5 were waited for; matrix products, arithmetic and copies ran while one was open for 9% of the time, Pallas kernels for 0%

profile of v9, /device:TPU:6, one launch (start us, length us, event | category | flops | bytes accessed | tf_op | source)
XLA Modules:
  0.0 319.3 jit_solution(13196162458329425057)
XLA Ops:
  0.0 0.0 copy-start
  0.0 5.4 %copy.14 = bf16[42,8,8,768]{3,2,1,0:T(8,128)(2,1)} copy(bf16[42,8,8,768]{3,1,2,0:T(8,128)(2,1)} %bitcast.51) | data formatting | bytes 8257536
  5.4 6.8 %copy.12 = bf16[112,3,8,768]{0,3,1,2:T(8,128)(2,1)} copy(bf16[112,3,8,768]{3,2,0,1:T(8,128)(2,1)} %bitcast.49) | data formatting | bytes 8257536 | tf_op jit(solution)/shard_map/reshape;squeeze | solution.py:89
  12.2 6.7 %copy.13 = bf16[8,112,2304]{2,1,0:T(8,128)(2,1)} copy(bf16[8,112,2304]{1,2,0:T(8,128)(2,1)} %bitcast.48) | data formatting | bytes 8257536 | tf_op jit(solution)/shard_map/reshape | solution.py:90
  18.8 8.1 %all-to-all-start = ((bf16[8,112,2304]{2,1,0:T(8,128)(2,1)}), bf16[8,112,2304]{2,1,0:T(8,128)(2,1)}, u32[]{:S(2)}, u32[]{:S(2)}) async-start(bf16[8,112,2304]{2,1,0:T(8,128)(2,1)} %copy.13), calls=%async_computation | async-start | bytes 8257536 | tf_op jit(solution)/shard_map/all_to_all | solution.py:91
  28.2 0.7 dynamic-slice_bitcast_fusion
  28.9 0.2 select_reduce_fusion
  29.1 0.1 broadcast_in_dim.38
  29.2 0.7 broadcast_in_dim_reshape.3.bias_ref
  29.9 57.3 %all-to-all-done.own_ref = bf16[8,112,2304]{2,1,0:T(8,128)(2,1)} async-done(((bf16[8,112,2304]{2,1,0:T(8,128)(2,1)}), bf16[8,112,2304]{2,1,0:T(8,128)(2,1)}, u32[]{:S(2)}, u32[]{:S(2)}) %all-to-all-start) | async-done | bytes 4128800 | tf_op jit(solution)/shard_map/all_to_all | solution.py:91
  87.2 26.4 %shard_map.82 = bf16[896,768]{1,0:T(8,128)(2,1)} custom-call(f32[1,1344]{1,0:T(1,128)} %broadcast_in_dim_reshape.3.bias_ref, bf16[8,112,2304]{2,1,0:T(8,128)(2,1)} %all-to-all-done.own_ref, bf16[2,2,1344,768]{3,2,1,0:T(8,128)(2,1)} %bitcast.46, bf16[2,2,1344,768]{3,2,1,0:T(8,128)(2,1)} %bitcast.47), custom_call_target="tpu_custom_call" | custom-call | tf_op jit(solution)/shard_map/pallas_call | solution.py:66
  113.5 5.9 %convolution_convert_fusion.1 = bf16[896,1536]{1,0:T(8,128)(2,1)} fusion(bf16[896,768]{1,0:T(8,128)(2,1)} %shard_map.82, bf16[1,768,6144]{2,1,0:T(8,128)(2,1)} %param.11), kind=kOutput, calls=%fused_computation.6 | convolution fusion | flops 2115305472 | bytes 6488064 | tf_op jit(solution)/shard_map/dot_general | solution.py:105
  119.4 6.9 %all-to-all-start.3 = ((bf16[8,112,1536]{2,1,0:T(8,128)(2,1)}), bf16[8,112,1536]{2,1,0:T(8,128)(2,1)S(1)}, u32[]{:S(2)}, u32[]{:S(2)}) async-start(bf16[8,112,1536]{2,1,0:T(8,128)(2,1)} %bitcast.53), calls=%async_computation.3 | async-start | bytes 5505024 | tf_op jit(solution)/shard_map/all_to_all | solution.py:107
  126.4 7.1 %convolution_convert_fusion.2 = bf16[896,2048]{1,0:T(8,128)(2,1)} fusion(bf16[896,768]{1,0:T(8,128)(2,1)} %shard_map.82, bf16[1,768,6144]{2,1,0:T(8,128)(2,1)} %param.11), kind=kOutput, calls=%fused_computation.7 | convolution fusion | flops 2820407296 | bytes 8192000 | tf_op jit(solution)/shard_map/dot_general | solution.py:105
  133.5 25.7 %all-to-all-done.3 = bf16[8,112,1536]{2,1,0:T(8,128)(2,1)S(1)} async-done(((bf16[8,112,1536]{2,1,0:T(8,128)(2,1)}), bf16[8,112,1536]{2,1,0:T(8,128)(2,1)S(1)}, u32[]{:S(2)}, u32[]{:S(2)}) %all-to-all-start.3) | async-done | bytes 2752544 | tf_op jit(solution)/shard_map/all_to_all | solution.py:107
  159.2 6.9 %all-to-all-start.2 = ((bf16[8,112,2048]{2,1,0:T(8,128)(2,1)}), bf16[8,112,2048]{2,1,0:T(8,128)(2,1)}, u32[]{:S(2)}, u32[]{:S(2)}) async-start(bf16[8,112,2048]{2,1,0:T(8,128)(2,1)} %bitcast.52), calls=%async_computation.2 | async-start | bytes 7340032 | tf_op jit(solution)/shard_map/all_to_all | solution.py:107
  166.1 8.3 %convolution_convert_fusion = bf16[896,2560]{1,0:T(8,128)(2,1)} fusion(bf16[896,768]{1,0:T(8,128)(2,1)} %shard_map.82, bf16[1,768,6144]{2,1,0:T(8,128)(2,1)} %param.11), kind=kOutput, calls=%fused_computation.3 | convolution fusion | flops 3525509120 | bytes 9895936 | tf_op jit(solution)/shard_map/dot_general | solution.py:105
  174.4 41.0 %all-to-all-done.2 = bf16[8,112,2048]{2,1,0:T(8,128)(2,1)} async-done(((bf16[8,112,2048]{2,1,0:T(8,128)(2,1)}), bf16[8,112,2048]{2,1,0:T(8,128)(2,1)}, u32[]{:S(2)}, u32[]{:S(2)}) %all-to-all-start.2) | async-done | bytes 3670048 | tf_op jit(solution)/shard_map/all_to_all | solution.py:107
  215.4 7.0 %all-to-all-start.1 = ((bf16[8,112,2560]{2,1,0:T(8,128)(2,1)}), bf16[8,112,2560]{2,1,0:T(8,128)(2,1)}, u32[]{:S(2)}, u32[]{:S(2)}) async-start(bf16[8,112,2560]{2,1,0:T(8,128)(2,1)} %bitcast.50), calls=%async_computation.1 | async-start | bytes 9175040 | tf_op jit(solution)/shard_map/all_to_all | solution.py:107
  222.5 0.0 copy-done
  222.5 1.3 fusion.9
  223.8 0.0 copy-start.1
  223.8 0.4 convert_reduce_fusion.2
  224.1 3.3 %convert_reduce_fusion.1 = f32[112,2048]{1,0:T(8,128)S(1)} fusion(bf16[8,112,2048]{2,1,0:T(8,128)(2,1)} %all-to-all-done.2), kind=kLoop, calls=%fused_computation.1 | loop fusion | flops 3440640 | bytes 4587520 | tf_op jit(solution)/shard_map/reduce_sum | solution.py:108
  227.5 0.0 copy-done.1
  227.5 2.2 fusion.7
  229.7 0.0 copy-start.2
  229.7 0.0 collective-permute-start.1
  229.7 51.2 %all-to-all-done.1 = bf16[8,112,2560]{2,1,0:T(8,128)(2,1)} async-done(((bf16[8,112,2560]{2,1,0:T(8,128)(2,1)}), bf16[8,112,2560]{2,1,0:T(8,128)(2,1)}, u32[]{:S(2)}, u32[]{:S(2)}) %all-to-all-start.1) | async-done | bytes 4587552 | tf_op jit(solution)/shard_map/all_to_all | solution.py:107
  280.9 0.0 copy-start.3
  280.9 3.2 %convert_reduce_fusion = f32[112,2560]{1,0:T(8,128)S(1)} fusion(bf16[8,112,2560]{2,1,0:T(8,128)(2,1)} %all-to-all-done.1), kind=kLoop, calls=%fused_computation | loop fusion | flops 4300800 | bytes 5734400 | tf_op jit(solution)/shard_map/reduce_sum | solution.py:108
  284.1 0.0 copy-done.2
  284.1 0.0 copy-done.3
  284.2 0.2 fusion.6
  284.4 0.1 collective-permute-start
  284.5 0.1 fusion.8
  284.6 13.1 %collective-permute-start.2 = (f32[112,1536]{1,0:T(8,128)S(1)}, f32[112,1536]{1,0:T(8,128)S(1)}, u32[]{:S(2)}, u32[]{:S(2)}) collective-permute-start(f32[112,1536]{1,0:T(8,128)S(1)} %fusion.8), channel_id=1, source_target_pairs={{0,8},{8,16},{16,24},{24,32},{32,40},{40,48},{48,56},{56,64},{64,7... | collective-permute-start | bytes 2064392 | tf_op jit(solution)/shard_map/ppermute | solution.py:19
  297.7 18.7 %collective-permute-done.2 = f32[112,1536]{1,0:T(8,128)S(1)} collective-permute-done((f32[112,1536]{1,0:T(8,128)S(1)}, f32[112,1536]{1,0:T(8,128)S(1)}, u32[]{:S(2)}, u32[]{:S(2)}) %collective-permute-start.2) | collective-permute-done | bytes 688160 | tf_op jit(solution)/shard_map/ppermute | solution.py:19
  316.4 0.0 collective-permute-done.1
  316.4 0.0 collective-permute-done
  316.4 2.9 maximum_bitcast_fusion
  (3 shorter events, 0.0 us)
Async XLA Ops:
  0.0 222.5 %copy-start = (f32[1,2,6144]{2,1,0:T(2,128)S(1)}, f32[1,2,6144]{2,1,0:T(2,128)}, u32[]{:S(2)}) copy-start(f32[1,2,6144]{2,1,0:T(2,128)} %param.12) | copy-start | bytes 147460
  18.8 68.3 %all-to-all-start = ((bf16[8,112,2304]{2,1,0:T(8,128)(2,1)}), bf16[8,112,2304]{2,1,0:T(8,128)(2,1)}, u32[]{:S(2)}, u32[]{:S(2)}) async-start(bf16[8,112,2304]{2,1,0:T(8,128)(2,1)} %copy.13), calls=%async_computation | async-start | bytes 8257536 | tf_op jit(solution)/shard_map/all_to_all | solution.py:91
  119.4 39.8 %all-to-all-start.3 = ((bf16[8,112,1536]{2,1,0:T(8,128)(2,1)}), bf16[8,112,1536]{2,1,0:T(8,128)(2,1)S(1)}, u32[]{:S(2)}, u32[]{:S(2)}) async-start(bf16[8,112,1536]{2,1,0:T(8,128)(2,1)} %bitcast.53), calls=%async_computation.3 | async-start | bytes 5505024 | tf_op jit(solution)/shard_map/all_to_all | solution.py:107
  159.2 56.2 %all-to-all-start.2 = ((bf16[8,112,2048]{2,1,0:T(8,128)(2,1)}), bf16[8,112,2048]{2,1,0:T(8,128)(2,1)}, u32[]{:S(2)}, u32[]{:S(2)}) async-start(bf16[8,112,2048]{2,1,0:T(8,128)(2,1)} %bitcast.52), calls=%async_computation.2 | async-start | bytes 7340032 | tf_op jit(solution)/shard_map/all_to_all | solution.py:107
  215.4 65.5 %all-to-all-start.1 = ((bf16[8,112,2560]{2,1,0:T(8,128)(2,1)}), bf16[8,112,2560]{2,1,0:T(8,128)(2,1)}, u32[]{:S(2)}, u32[]{:S(2)}) async-start(bf16[8,112,2560]{2,1,0:T(8,128)(2,1)} %bitcast.50), calls=%async_computation.1 | async-start | bytes 9175040 | tf_op jit(solution)/shard_map/all_to_all | solution.py:107
  223.8 3.7 %copy-start.1 = (f32[112,6144]{1,0:T(8,128)}, f32[112,6144]{1,0:T(8,128)S(1)}, u32[]{:S(2)}) copy-start(f32[112,6144]{1,0:T(8,128)S(1)} %fusion.9) | copy-start | bytes 8257540
  229.7 54.4 %copy-start.2 = (f32[112,6144]{1,0:T(8,128)S(1)}, f32[112,6144]{1,0:T(8,128)}, u32[]{:S(2)}) copy-start(f32[112,6144]{1,0:T(8,128)} %copy-done.1) | copy-start | bytes 8257540
  229.7 86.7 %collective-permute-start.1 = (f32[112,2048]{1,0:T(8,128)}, f32[112,2048]{1,0:T(8,128)}, u32[]{:S(2)}, u32[]{:S(2)}) collective-permute-start(f32[112,2048]{1,0:T(8,128)} %fusion.7), channel_id=1, source_target_pairs={{0,8},{8,16},{16,24},{24,32},{32,40},{40,48},{48,56},{56,64},{64,7... | collective-permute-start | bytes 2752520 | tf_op jit(solution)/shard_map/ppermute | solution.py:19
  280.9 3.3 %copy-start.3 = (f32[1,112,6144]{2,1,0:T(8,128)S(1)}, f32[1,112,6144]{2,1,0:T(8,128)}, u32[]{:S(2)}) copy-start(f32[1,112,6144]{2,1,0:T(8,128)} %param.8) | copy-start | bytes 8257540
  284.4 32.0 %collective-permute-start = (f32[112,2560]{1,0:T(8,128)S(1)}, f32[112,2560]{1,0:T(8,128)S(1)}, u32[]{:S(2)}, u32[]{:S(2)}) collective-permute-start(f32[112,2560]{1,0:T(8,128)S(1)} %fusion.6), channel_id=1, source_target_pairs={{0,8},{8,16},{16,24},{24,32},{32,40},{40,48},{48,56},{56,64},{64,7... | collective-permute-start | bytes 3440648 | tf_op jit(solution)/shard_map/ppermute | solution.py:19
  284.6 31.8 %collective-permute-start.2 = (f32[112,1536]{1,0:T(8,128)S(1)}, f32[112,1536]{1,0:T(8,128)S(1)}, u32[]{:S(2)}, u32[]{:S(2)}) collective-permute-start(f32[112,1536]{1,0:T(8,128)S(1)} %fusion.8), channel_id=1, source_target_pairs={{0,8},{8,16},{16,24},{24,32},{32,40},{40,48},{48,56},{56,64},{64,7... | collective-permute-start | bytes 2064392 | tf_op jit(solution)/shard_map/ppermute | solution.py:19
